TPU v7x, 256 devices: a whole 4x4x8 slice. The times are simulated.
256 devices in a mesh: group: 32 (over z, y), tensor: 8 (over x, core).
Axes of the slice: x: 4, y: 4, z: 8, core: 2. Of those that a mesh axis runs over, the one named last changes fastest.
Arguments:
- query: bfloat16 [2, 1024, 2048], P(None, 'group', 'tensor'), may hold values from -80 to 80
- self_kv: bfloat16 [2, 1024, 2, 2048], P(None, 'group', None, 'tensor'), may hold values from -6 to 6
- kv_pages: bfloat16 [2, 1536, 16, 2, 2048], P(None, 'group', None, None, 'tensor'), may hold values from -6 to 6
- page_dest: int32 [1536, 1], replicated, may hold values from 0 to 31; in each aligned block of 48 rows (0 to 47, 48 to 95, ...) at most 3 rows name the same one
- page_request: int32 [1536], replicated, may hold values from 0 to 1
- score_len: int32 [64], P('group'), may hold values from 1 to 16
- out_proj: bfloat16 [2, 2048, 2048], P(None, 'tensor'), may hold values from -0.125 to 0.125
- residual: bfloat16 [2, 1024, 2048], P(None, ('group', 'tensor')), may hold values from -6 to 6
- norm_gain: float32 [2, 2048], replicated, may hold values from 0.5 to 40
- norm_bias: float32 [2, 2048], replicated, may hold values from -3 to 3
- vocab: bfloat16 [2, 2048, 196608], P(None, None, ('group', 'tensor')), may hold values from -0.3984375 to 0.3984375
- targets: int32 [1024], replicated, may hold values from 0 to 196607
Outputs:
- logprob: float32 [2, 1024], P(None, ('group', 'tensor'))
Inputs may be any that keep to these rules, and one draw needn't show every extreme that they name: `page_dest`: the 48 pages of each aligned block (pages held by one group) go to any one group at most 3 times; some block sends exactly 3 to some group.
All inputs are finite; a program needn't handle non-finite values.
Results may differ from a plain program's by a relative error of at most 0.00097.
Values may be sent and summed in bfloat16 or wider, within the bound.
No kernel may reach another device: no remote copies, remote signals or barrier semaphores. Data moves between devices by JAX's collectives and lax.ppermute only.
A program may use at most 128 MiB of HBM per device.

v0:
```python
import math

import jax
import jax.numpy as jnp
from jax import lax
from jax.sharding import PartitionSpec as P

HEADS = 16
HEAD_DIM = 128
REQ_GRP = 2
SCORE_LEN = 16


NEGATIVE = -1e30
EPSILON = 1e-05


def route_tables(destination, request, groups, per_owner, capacity, requests):
    page_count = destination.shape[0]
    owner_group = jnp.arange(page_count, dtype=jnp.int32) // per_owner
    columns = jnp.arange(groups, dtype=jnp.int32)
    onehot = (destination[:, None] == columns[None, :]).astype(jnp.int32)
    within = jnp.cumsum(onehot.reshape(groups, per_owner, groups), axis=1).reshape(
        page_count, groups
    )
    position = jnp.sum(within * onehot, axis=1) - 1
    arrival = owner_group * capacity + position
    combined = destination * requests + request
    pair_hot = (
        combined[:, None] == jnp.arange(groups * requests, dtype=jnp.int32)[None, :]
    ).astype(jnp.int32)
    running = jnp.cumsum(pair_hot, axis=0)
    page_rank = jnp.sum(running * pair_hot, axis=1) - 1
    totals = running[-1].reshape(groups, requests)
    return (position, arrival, page_rank, totals)


def alibi_slopes(head_count):
    return jnp.exp2(-8.0 * jnp.arange(1, head_count + 1).astype(jnp.float32) / head_count)


def per_device(
    query,
    self_kv,
    kv_pages,
    page_dest,
    page_request,
    score_len,
    out_proj,
    residual,
    norm_gain,
    norm_bias,
    vocab,
    targets,
):
    groups = lax.axis_size("group")
    shards = lax.axis_size("tensor")
    group_id = lax.axis_index("group")
    tensor_id = lax.axis_index("tensor")
    tok_grp = query.shape[1]
    flat_width = query.shape[2]
    head_local = flat_width // HEAD_DIM
    per_owner = kv_pages.shape[1]
    page_len = kv_pages.shape[2]
    capacity = 2 * per_owner // groups
    destination = page_dest[:, 0]
    page_total = destination.shape[0]
    position, arrival, page_rank, totals = route_tables(
        destination, page_request, groups, per_owner, capacity, REQ_GRP
    )
    slopes = lax.dynamic_slice_in_dim(alibi_slopes(HEADS), tensor_id * head_local, head_local)
    score_scale = 1.0 / math.sqrt(HEAD_DIM)
    queries = query.reshape(2, tok_grp, head_local, HEAD_DIM)
    own_keys = self_kv[:, :, 0].reshape(2, tok_grp, head_local, HEAD_DIM)
    own_values = self_kv[:, :, 1].reshape(2, tok_grp, head_local, HEAD_DIM)
    token_ids = jnp.arange(tok_grp, dtype=jnp.int32)
    token_request = token_ids // SCORE_LEN
    token_step = token_ids % SCORE_LEN
    own_distance = (token_step[:, None] - token_step[None, :]).astype(jnp.float32)
    own_scores = (
        jnp.einsum("mthd,mshd->mhts", queries, own_keys, preferred_element_type=jnp.float32)
        * score_scale
    )
    own_scores = own_scores - slopes[None, :, None, None] * own_distance[None, None]
    own_allowed = (
        (token_request[:, None] == token_request[None, :])
        & (token_step[None, :] <= token_step[:, None])
    )[None, None]
    own_scores = jnp.where(own_allowed, own_scores, NEGATIVE)
    own_top = jnp.max(own_scores, -1)
    my_dest = lax.dynamic_slice_in_dim(destination, group_id * per_owner, per_owner)
    my_position = lax.dynamic_slice_in_dim(position, group_id * per_owner, per_owner)
    buffer = groups * capacity
    outgoing = jnp.zeros((2, buffer, page_len, 2, flat_width), jnp.bfloat16)
    outgoing = outgoing.at[:, my_dest * capacity + my_position].set(kv_pages)
    incoming = lax.all_to_all(outgoing, "group", split_axis=1, concat_axis=1, tiled=True)
    target_place = jnp.where(destination == group_id, arrival, buffer)
    slot_index = (
        jnp.full((buffer,), page_total, jnp.int32)
        .at[target_place]
        .set(jnp.arange(page_total, dtype=jnp.int32), mode="drop")
    )
    is_valid = slot_index < page_total
    safe_index = jnp.minimum(slot_index, page_total - 1)
    key_data = incoming[:, :, :, 0].reshape(2, buffer * page_len, head_local, HEAD_DIM)
    values = incoming[:, :, :, 1].reshape(2, buffer * page_len, head_local, HEAD_DIM)
    key_request = jnp.repeat(jnp.where(is_valid, page_request[safe_index], -1), page_len)
    key_position = (
        page_rank[safe_index][:, None] * page_len + jnp.arange(page_len, dtype=jnp.int32)[None, :]
    ).reshape(-1)
    context = totals[group_id][token_request] * page_len
    distance = ((context + token_step)[:, None] - key_position[None, :]).astype(jnp.float32)
    scores = (
        jnp.einsum("mthd,mkhd->mhtk", queries, key_data, preferred_element_type=jnp.float32)
        * score_scale
    )
    scores = scores - slopes[None, :, None, None] * distance[None, None]
    allowed = (key_request[None, :] == token_request[:, None])[None, None]
    scores = jnp.where(allowed, scores, NEGATIVE)
    row_top = jnp.maximum(jnp.max(scores, -1), own_top)
    exp_terms = jnp.where(allowed, jnp.exp(scores - row_top[..., None]), 0.0)
    denominator = jnp.sum(exp_terms, -1)
    numerator = jnp.einsum(
        "mhtk,mkhd->mthd",
        exp_terms.astype(jnp.bfloat16),
        values,
        preferred_element_type=jnp.float32,
    )
    own_terms = jnp.where(own_allowed, jnp.exp(own_scores - row_top[..., None]), 0.0)
    denominator = denominator + jnp.sum(own_terms, -1)
    numerator = numerator + jnp.einsum(
        "mhts,mshd->mthd",
        own_terms.astype(jnp.bfloat16),
        own_values,
        preferred_element_type=jnp.float32,
    )
    attended = (
        (numerator / jnp.transpose(denominator, (0, 2, 1))[..., None])
        .reshape(2, tok_grp, flat_width)
        .astype(jnp.bfloat16)
    )
    rows_local = tok_grp // shards
    mixed = lax.psum_scatter(
        jnp.einsum("mtk,mkd->tmd", attended, out_proj, preferred_element_type=jnp.float32),
        "tensor",
        scatter_dimension=0,
        tiled=True,
    )
    hidden = residual.astype(jnp.float32) + jnp.transpose(mixed, (1, 0, 2))
    row_mean = jnp.mean(hidden, axis=-1, keepdims=True)
    centered = hidden - row_mean
    variance = jnp.mean(centered * centered, axis=-1, keepdims=True)
    normed = (
        centered / jnp.sqrt(variance + EPSILON) * norm_gain[:, None, :] + norm_bias[:, None, :]
    ).astype(jnp.bfloat16)
    voc_local = vocab.shape[2]
    offset = (group_id * shards + tensor_id) * voc_local
    logits = jnp.einsum(
        "mnd,mdv->mnv",
        lax.all_gather(normed, ("group", "tensor"), axis=1, tiled=True),
        vocab,
        preferred_element_type=jnp.float32,
    )
    row_peak = lax.pmax(jnp.max(logits, axis=2), ("group", "tensor"))
    wanted = targets - offset
    inside = (wanted >= 0) & (wanted < voc_local)
    picked = jnp.take_along_axis(logits, jnp.clip(wanted, 0, voc_local - 1)[None, :, None], axis=2)[
        ..., 0
    ]
    exp_total, chosen = lax.psum(
        (
            jnp.sum(jnp.exp(logits - row_peak[..., None]), axis=2),
            jnp.where(inside[None, :], picked, 0.0),
        ),
        ("group", "tensor"),
    )
    logprob_all = chosen - (row_peak + jnp.log(exp_total))
    mine = lax.dynamic_slice_in_dim(
        logprob_all, group_id * tok_grp + tensor_id * rows_local, rows_local, 1
    )
    local_ids = tensor_id * rows_local + jnp.arange(rows_local, dtype=jnp.int32)
    keep_token = local_ids % SCORE_LEN < score_len[local_ids // SCORE_LEN]
    return jnp.where(keep_token[None, :], mine, 0.0)


def solution(mesh):
    in_specs = (
        P(None, "group", "tensor"),
        P(None, "group", None, "tensor"),
        P(None, "group", None, None, "tensor"),
        P(),
        P(),
        P("group"),
        P(None, "tensor", None),
        P(None, ("group", "tensor"), None),
        P(),
        P(),
        P(None, None, ("group", "tensor")),
        P(),
    )
    out_specs = P(None, ("group", "tensor"))
    return jax.shard_map(
        per_device, mesh=mesh, in_specs=in_specs, out_specs=out_specs, check_vma=False
    )
```

profile of v0, /device:TPU:1, one launch (start us, length us, event | category | flops | bytes accessed | tf_op | source)
XLA Modules:
  0.0 520.5 jit_solution(7488796929031193324)
XLA Ops:
  6.5 0.9 reduce.1
  7.4 0.1 eq.93
  7.5 0.1 copy.75
  7.6 1.3 select_reduce_fusion
  9.0 0.1 sub.123
  9.0 2.9 copy.77
  11.9 0.1 compare_select_fusion.5
  12.0 2.1 broadcast_in_dim.127
  14.1 7.7 %scatter_fusion = bf16[2,96,16,2,256]{4,2,3,1,0:T(8,128)(2,1)} fusion(bf16[2,96,16,2,256]{4,2,3,1,0:T(8,128)(2,1)} %broadcast_in_dim.127, s32[48]{0:T(128)S(1)} %compare_select_fusion.5, bf16[48,2,16,2,256]{4,2,3,1,0:T(8,128)(2,1)} %copy.77), kind=kCustom, calls=%fused_computation.4 | custom fusion | bytes 4718784 | tf_op jit(solution)/shard_map/scatter | solution.py:95
  21.8 4.0 copy.78
  25.9 12.3 %all-to-all-start = ((bf16[2,96,16,2,256]{4,2,3,0,1:T(8,128)(2,1)}), bf16[2,96,16,2,256]{4,2,3,0,1:T(8,128)(2,1)}, u32[]{:S(2)}, u32[]{:S(2)}) async-start(bf16[2,96,16,2,256]{4,2,3,0,1:T(8,128)(2,1)} %copy.78), calls=%async_computation | async-start | bytes 6291456 | tf_op jit(solution)/shard_map/all_to_all | solution.py:96
  38.2 0.1 sub.125
  38.4 18.1 %reduce-window.6 = s32[64,12,128]{2,1,0:T(8,128)S(1)} reduce-window(s32[64,12,128]{2,1,0:T(8,128)S(1)} %fusion.29, s32[]{:T(128)} %constant.134.clone.1), window={size=1x1x128 pad=0_0x0_0x127_0}, to_apply=%region_4.5 | reduce-window | flops 12484608 | bytes 786436 | tf_op jit(solution)/shard_map/reduce-window
  56.5 0.2 slice.43
  56.8 0.3 copy.83
  57.1 0.1 copy.84
  57.2 0.2 broadcast_add_fusion
  57.4 0.2 select_reduce_fusion.1
  57.5 0.2 slice_reduce_fusion.2
  57.7 0.1 reshape_squeeze.17
  57.8 6.2 %scatter_custom_fusion.1 = s32[96]{0:T(128)S(1)} fusion(s32[1536]{0:T(1024)S(1)} %get-tuple-element.7, s32[1536]{0:T(1024)S(1)} %iota.68, s32[]{:T(128)} %constant.147.clone.1), kind=kCustom, calls=%fused_computation.143 | custom fusion | bytes 388 | tf_op jit(solution)/shard_map/scatter | solution.py:101
  64.0 1.1 gather_fusion.1
  65.2 1.1 gather_fusion.2
  66.4 0.1 iota_add_fusion
  66.4 0.1 add.270
  66.5 0.1 broadcast_in_dim.132
  66.6 0.1 eq.99
  66.7 0.1 dynamic_slice.17
  66.8 0.6 fusion.77
  67.4 1.2 fusion.66
  68.6 0.3 slice_reduce_fusion
  68.9 0.1 compare_and_fusion
  69.1 0.1 broadcast_multiply_fusion.1
  69.1 0.2 fusion.79
  69.3 0.1 broadcast_compare_fusion
  69.4 0.1 subtract_convert_fusion
  69.5 0.1 broadcast_multiply_fusion
  69.6 38.9 %all-to-all-done = bf16[2,96,16,2,256]{4,2,3,0,1:T(8,128)(2,1)} async-done(((bf16[2,96,16,2,256]{4,2,3,0,1:T(8,128)(2,1)}), bf16[2,96,16,2,256]{4,2,3,0,1:T(8,128)(2,1)}, u32[]{:S(2)}, u32[]{:S(2)}) %all-to-all-start) | async-done | bytes 3145760 | tf_op jit(solution)/shard_map/all_to_all | solution.py:96
  108.5 3.4 fusion.76
  111.8 1.3 copy.80
  113.1 3.5 reshape_squeeze.16
  116.6 2.3 fusion.78
  118.9 0.3 fusion.27
  119.2 0.2 convolution_bitcast_fusion.1
  119.4 1.3 copy.79
  120.7 3.5 reshape_squeeze.15
  124.2 1.9 fusion.22
  126.1 1.3 convolution_bitcast_fusion
  127.4 0.2 all-gather.2.cloned.1.call-start
  127.7 0.6 dynamic-slice.1
  128.9 62.4 %all-reduce.4.cloned.1.call-done = f32[32,2,2048]{2,0,1:T(8,128)} async-done(((f32[32,2,2048]{2,0,1:T(8,128)}), f32[32,2,2048]{2,0,1:T(8,128)}) %all-reduce.4.cloned.1.call-update) | async-done | bytes 524304
  191.4 1.0 fusion.58
  192.4 1.1 multiply_reduce_fusion
  193.5 1.0 add_convert_fusion
  194.5 0.6 copy.91
  195.2 0.6 gather_fusion
  195.9 119.5 %all-gather.2.cloned.1.call-done = bf16[2,1024,2048]{2,0,1:T(2,128)(2,1)} async-done(((bf16[2,4,2048]{2,0,1:T(2,128)(2,1)}), bf16[2,1024,2048]{2,0,1:T(2,128)(2,1)}) %all-gather.2.cloned.1.call-update) | async-done | bytes 8388624 | tf_op jit(solution)/shard_map/all_gather | solution.py:160
  315.4 23.1 %fusion.80 = (f32[2,1024]{1,0:T(2,128)S(1)}, f32[2,1024,768]{1,2,0:T(8,128)}) fusion(bf16[2,2048,768]{2,1,0:T(8,128)(2,1)} %param.22, bf16[2,1024,2048]{2,0,1:T(2,128)(2,1)} %all-gather.2.cloned.1.call-done), kind=kOutput, calls=%fused_computation.151 | convolution fusion | flops 6444021760 | bytes 20979712 | tf_op jit(solution)/shard_map/mnd,mdv->mnv/dot_general | solution.py:158
  338.5 10.4 %copy.94 = f32[2,1024,768]{2,0,1:T(2,128)} copy(f32[2,1024,768]{1,2,0:T(8,128)} %get-tuple-element.25) | data formatting | bytes 12582912 | tf_op jit(solution)/shard_map/mnd,mdv->mnv/dot_general | solution.py:158
  348.9 74.5 %pmax.7 = f32[2,1024]{1,0:T(2,128)S(1)} all-reduce(f32[2,1024]{1,0:T(2,128)S(1)} %get-tuple-element.24), channel_id=1, replica_groups=mesh['group'=32,'tensor'=8] {'group','tensor'}, use_global_device_ids=true, to_apply=%region_16.17 | all-reduce | flops 2048 | bytes 16384 | tf_op jit(solution)/shard_map/pmax | solution.py:164
  423.4 3.6 exponential_reduce_fusion
  427.0 12.2 %gather_fusion.3 = f32[1024,2]{0,1:T(2,128)S(1)} fusion(f32[2,1024,768]{2,0,1:T(2,128)} %copy.94, s32[1024]{0:T(1024)S(1)} %bitcast.111), kind=kCustom, calls=%fused_computation.3 | custom fusion | bytes 24576 | tf_op jit(solution)/shard_map/jit(take_along_axis)/gather | solution.py:167
  439.2 73.8 %all-reduce.1 = (f32[2,1024]{1,0:T(2,128)S(1)}, f32[2,1024]{1,0:T(2,128)S(1)}) all-reduce(f32[2,1024]{1,0:T(2,128)S(1)} %exponential_reduce_fusion, f32[2,1024]{1,0:T(2,128)S(1)} %select_bitcast_fusion), channel_id=1, replica_groups=mesh['group'=32,'tensor'=8] {'group','tensor'}, use_global_device_ids=true, to_apply=%region_18.19 | all-reduce | flops 4096 | bytes 32768 | tf_op jit(solution)/shard_map/psum | solution.py:170
  513.0 0.6 fusion.61
  (56 shorter events, 0.6 us)
Async XLA Ops:
  6.5 119.5 %copy-start = (bf16[2,256,2048]{2,1,0:T(8,128)(2,1)S(1)}, bf16[2,256,2048]{2,1,0:T(8,128)(2,1)}, u32[]{:S(2)}) copy-start(bf16[2,256,2048]{2,1,0:T(8,128)(2,1)} %param.18) | copy-start | bytes 6291460
  6.5 5.4 %copy-start.7 = (s32[1536,1]{0,1:T(1,128)S(1)}, s32[1536,1]{0,1:T(1,128)}, u32[]{:S(2)}) copy-start(s32[1536,1]{0,1:T(1,128)} %param.15) | copy-start | bytes 18436
  25.9 12.5 %copy-start.2 = (s32[1536]{0:T(1024)S(1)}, s32[1536]{0:T(1024)}, u32[]{:S(2)}) copy-start(s32[1536]{0:T(1024)} %param.16) | copy-start | bytes 18436
  25.9 82.6 %all-to-all-start = ((bf16[2,96,16,2,256]{4,2,3,0,1:T(8,128)(2,1)}), bf16[2,96,16,2,256]{4,2,3,0,1:T(8,128)(2,1)}, u32[]{:S(2)}, u32[]{:S(2)}) async-start(bf16[2,96,16,2,256]{4,2,3,0,1:T(8,128)(2,1)} %copy.78), calls=%async_computation | async-start | bytes 6291456 | tf_op jit(solution)/shard_map/all_to_all | solution.py:96
  38.1 153.2 %all-reduce.4.cloned.1.call-start = ((), (), s32[]{:S(2)}) async-start(), calls=%async_computation.2 | async-start | bytes 1048576
  56.8 11.9 %copy-start.5 = (bf16[2,32,2,256]{3,2,1,0:T(2,128)(2,1)S(1)}, bf16[2,32,2,256]{3,2,1,0:T(2,128)(2,1)}, u32[]{:S(2)}) copy-start(bf16[2,32,2,256]{3,2,1,0:T(2,128)(2,1)} %param.13) | copy-start | bytes 196612
  56.8 12.4 %copy-start.6 = (bf16[2,32,256]{2,1,0:T(8,128)(2,1)S(1)}, bf16[2,32,256]{2,1,0:T(8,128)(2,1)}, u32[]{:S(2)}) copy-start(bf16[2,32,256]{2,1,0:T(8,128)(2,1)} %param.12) | copy-start | bytes 98308
  116.6 2.8 copy-start.3
  126.1 1.6 copy-start.11
  126.1 65.3 %copy-start.4 = (bf16[2,4,2048]{2,1,0:T(4,128)(2,1)S(1)}, bf16[2,4,2048]{2,1,0:T(4,128)(2,1)}, u32[]{:S(2)}) copy-start(bf16[2,4,2048]{2,1,0:T(4,128)(2,1)} %param.19) | copy-start | bytes 98308
  126.1 67.4 %copy-start.8 = (f32[2,2048]{1,0:T(2,128)S(1)}, f32[2,2048]{1,0:T(2,128)}, u32[]{:S(2)}) copy-start(f32[2,2048]{1,0:T(2,128)} %param.21) | copy-start | bytes 49156
  126.1 67.4 %copy-start.9 = (f32[2,2048]{1,0:T(2,128)S(1)}, f32[2,2048]{1,0:T(2,128)}, u32[]{:S(2)}) copy-start(f32[2,2048]{1,0:T(2,128)} %param.20) | copy-start | bytes 49156
  126.1 69.1 %copy-start.1 = (s32[2]{0:T(128)S(1)}, s32[2]{0:T(128)}, u32[]{:S(2)}) copy-start(s32[2]{0:T(128)} %param.17) | copy-start | bytes 28
  126.1 69.7 %copy-start.10 = (s32[1024]{0:T(1024)S(1)}, s32[1024]{0:T(1024)}, u32[]{:S(2)}) copy-start(s32[1024]{0:T(1024)} %param.23) | copy-start | bytes 12292
  127.4 188.0 %all-gather.2.cloned.1.call-start = ((), (), s32[]{:S(2)}) async-start(), calls=%async_computation.1 | async-start | bytes 8421376 | tf_op jit(solution)/shard_map/all_gather | solution.py:160
Sparse Core Ops, SparseCore 0:
  127.6 63.7 all-reduce.3
  195.5 119.8 all-gather.1
where the time goes:
time: 522 us; the launch traced here: 521 us
  waiting for transfers between devices  221 us (42%)
  blocking collectives  148 us (28%)
  local copies, waits for them, and re-layouts  65 us (12%)
  other arithmetic  30.6 us (6%)
  matrix products  28.9 us (6%)
  between operations  14.5 us (3%)
  starting transfers between devices  12.5 us (2%)
    all_gather x1, waiting for transfers between devices, per_device(): lax.all_gather(normed, ('group', 'tensor'), axis=1, tiled=True)  119 us
    pmax x1, blocking collectives, per_device(): row_peak = lax.pmax(jnp.max(logits, axis=2), ('group', 'tensor'))  74.5 us
    psum x1, blocking collectives, per_device(): lax.psum((jnp.sum(jnp.exp(logits - row_peak[..., None]), axis=2), jnp.whe...  73.8 us
    unnamed x3, waiting for transfers between devices  62.5 us
    all_to_all x1, waiting for transfers between devices, per_device(): lax.all_to_all(outgoing, 'group', split_axis=1, concat_axis=1, tiled=True)  38.9 us
    dot_general x1, matrix products, per_device(): jnp.einsum('mnd,mdv->mnv', lax.all_gather(normed, ('group', 'tensor'), ax...  23.1 us
    another operation x3, other arithmetic  18.4 us
    all_to_all x1, starting transfers between devices, per_device(): lax.all_to_all(outgoing, 'group', split_axis=1, concat_axis=1, tiled=True)  12.3 us
  transfers between devices with their start and end apart: 3, of which 3 were waited for; matrix products, arithmetic and copies ran while one was open for 6% of the time, Pallas kernels for 0%

commit v1 on v0

v1 whole, which is shorter than its diff:
```python
import math

import jax
import jax.numpy as jnp
from jax import lax
from jax.sharding import PartitionSpec as P

HEADS = 16
HEAD_DIM = 128
REQ_GRP = 2
SCORE_LEN = 16


NEGATIVE = -1e30
EPSILON = 1e-05


def alibi_slopes(head_count):
    return jnp.exp2(-8.0 * jnp.arange(1, head_count + 1).astype(jnp.float32) / head_count)


def lse_combine(peak, total, chosen, axis):
    top = jnp.max(peak, axis=axis, keepdims=True)
    total = jnp.sum(total * jnp.exp(peak - top), axis=axis)
    return jnp.squeeze(top, axis), total, jnp.sum(chosen, axis=axis)


def per_device(
    query,
    self_kv,
    kv_pages,
    page_dest,
    page_request,
    score_len,
    out_proj,
    residual,
    norm_gain,
    norm_bias,
    vocab,
    targets,
):
    groups = lax.axis_size("group")
    shards = lax.axis_size("tensor")
    group_id = lax.axis_index("group")
    tensor_id = lax.axis_index("tensor")
    tok_grp = query.shape[1]
    flat_width = query.shape[2]
    head_local = flat_width // HEAD_DIM
    per_owner = kv_pages.shape[1]
    page_len = kv_pages.shape[2]
    capacity = 2 * per_owner // groups
    destination = page_dest[:, 0]
    page_total = destination.shape[0]
    buffer = groups * capacity
    width = residual.shape[2]

    local = jnp.arange(per_owner, dtype=jnp.int32)
    earlier = local[None, :] < local[:, None]
    my_dest = lax.dynamic_slice_in_dim(destination, group_id * per_owner, per_owner)
    my_position = jnp.sum(
        ((my_dest[None, :] == my_dest[:, None]) & earlier).astype(jnp.int32), axis=1
    )
    out_slot = my_dest * capacity + my_position
    slots = jnp.arange(buffer, dtype=jnp.int32)
    send_hot = out_slot[None, :] == slots[:, None]
    send_from = jnp.sum(jnp.where(send_hot, local[None, :], 0), axis=1)
    outgoing = jnp.take(kv_pages, send_from, axis=1)
    incoming = lax.all_to_all(outgoing, "group", split_axis=1, concat_axis=1, tiled=True)

    pages = jnp.arange(page_total, dtype=jnp.int32)
    mine = destination == group_id
    mine_blocks = mine.reshape(groups, per_owner)
    rank_in_block = jnp.sum(
        (mine_blocks[:, None, :] & earlier[None]).astype(jnp.int32), axis=2
    ).reshape(-1)
    arrival = (pages // per_owner) * capacity + rank_in_block
    recv_hot = mine[None, :] & (arrival[None, :] == slots[:, None])
    is_valid = jnp.any(recv_hot, axis=1)
    slot_page = jnp.sum(jnp.where(recv_hot, pages[None, :], 0), axis=1)
    slot_request = jnp.sum(jnp.where(recv_hot, page_request[None, :], 0), axis=1)
    slot_rank = jnp.sum(
        (
            mine[None, :]
            & (page_request[None, :] == slot_request[:, None])
            & (pages[None, :] < slot_page[:, None])
        ).astype(jnp.int32),
        axis=1,
    )
    request_ids = jnp.arange(REQ_GRP, dtype=jnp.int32)
    totals = jnp.sum(
        (mine[None, :] & (page_request[None, :] == request_ids[:, None])).astype(jnp.int32),
        axis=1,
    )

    slopes = lax.dynamic_slice_in_dim(alibi_slopes(HEADS), tensor_id * head_local, head_local)
    score_scale = 1.0 / math.sqrt(HEAD_DIM)
    queries = query.reshape(2, tok_grp, head_local, HEAD_DIM)
    own_keys = self_kv[:, :, 0].reshape(2, tok_grp, head_local, HEAD_DIM)
    own_values = self_kv[:, :, 1].reshape(2, tok_grp, head_local, HEAD_DIM)
    token_ids = jnp.arange(tok_grp, dtype=jnp.int32)
    token_request = token_ids // SCORE_LEN
    token_step = token_ids % SCORE_LEN
    own_distance = (token_step[:, None] - token_step[None, :]).astype(jnp.float32)
    own_scores = (
        jnp.einsum("mthd,mshd->mhts", queries, own_keys, preferred_element_type=jnp.float32)
        * score_scale
    )
    own_scores = own_scores - slopes[None, :, None, None] * own_distance[None, None]
    own_allowed = (
        (token_request[:, None] == token_request[None, :])
        & (token_step[None, :] <= token_step[:, None])
    )[None, None]
    own_scores = jnp.where(own_allowed, own_scores, NEGATIVE)
    own_top = jnp.max(own_scores, -1)

    key_data = incoming[:, :, :, 0].reshape(2, buffer * page_len, head_local, HEAD_DIM)
    values = incoming[:, :, :, 1].reshape(2, buffer * page_len, head_local, HEAD_DIM)
    key_request = jnp.repeat(jnp.where(is_valid, slot_request, -1), page_len)
    key_position = (
        slot_rank[:, None] * page_len + jnp.arange(page_len, dtype=jnp.int32)[None, :]
    ).reshape(-1)
    context = totals[token_request] * page_len
    distance = ((context + token_step)[:, None] - key_position[None, :]).astype(jnp.float32)
    scores = (
        jnp.einsum("mthd,mkhd->mhtk", queries, key_data, preferred_element_type=jnp.float32)
        * score_scale
    )
    scores = scores - slopes[None, :, None, None] * distance[None, None]
    allowed = (key_request[None, :] == token_request[:, None])[None, None]
    scores = jnp.where(allowed, scores, NEGATIVE)
    row_top = jnp.maximum(jnp.max(scores, -1), own_top)
    exp_terms = jnp.where(allowed, jnp.exp(scores - row_top[..., None]), 0.0)
    denominator = jnp.sum(exp_terms, -1)
    numerator = jnp.einsum(
        "mhtk,mkhd->mthd",
        exp_terms.astype(jnp.bfloat16),
        values,
        preferred_element_type=jnp.float32,
    )
    own_terms = jnp.where(own_allowed, jnp.exp(own_scores - row_top[..., None]), 0.0)
    denominator = denominator + jnp.sum(own_terms, -1)
    numerator = numerator + jnp.einsum(
        "mhts,mshd->mthd",
        own_terms.astype(jnp.bfloat16),
        own_values,
        preferred_element_type=jnp.float32,
    )
    attended = (
        (numerator / jnp.transpose(denominator, (0, 2, 1))[..., None])
        .reshape(2, tok_grp, flat_width)
        .astype(jnp.bfloat16)
    )

    rows_local = tok_grp // shards
    partial = jnp.einsum("mtk,mkd->tmd", attended, out_proj, preferred_element_type=jnp.float32)
    parts = lax.all_to_all(
        partial.reshape(shards, rows_local, 2, width), "tensor", 0, 0, tiled=True
    )
    mixed = jnp.sum(parts, axis=0)
    hidden = residual.astype(jnp.float32) + jnp.transpose(mixed, (1, 0, 2))
    row_mean = jnp.mean(hidden, axis=-1, keepdims=True)
    centered = hidden - row_mean
    variance = jnp.mean(centered * centered, axis=-1, keepdims=True)
    normed = (
        centered / jnp.sqrt(variance + EPSILON) * norm_gain[:, None, :] + norm_bias[:, None, :]
    ).astype(jnp.bfloat16)

    voc_local = vocab.shape[2]
    offset = (group_id * shards + tensor_id) * voc_local
    everyone = lax.all_gather(normed, ("group", "tensor"), axis=1, tiled=True)
    logits = jnp.einsum("mnd,mdv->mnv", everyone, vocab, preferred_element_type=jnp.float32)
    local_peak = jnp.max(logits, axis=2)
    local_total = jnp.sum(jnp.exp(logits - local_peak[..., None]), axis=2)
    wanted = targets - offset
    hit = jnp.arange(voc_local, dtype=jnp.int32)[None, None, :] == wanted[None, :, None]
    local_chosen = jnp.sum(jnp.where(hit, logits, 0.0), axis=2)

    stats = jnp.stack([local_peak, local_total, local_chosen]).reshape(
        3, 2, groups, shards, rows_local
    )
    stats = lax.all_to_all(stats, "tensor", 3, 3, tiled=True)
    peak, total, chosen = lse_combine(stats[0], stats[1], stats[2], 2)
    stats = lax.all_to_all(jnp.stack([peak, total, chosen]), "group", 2, 2, tiled=True)
    peak, total, chosen = lse_combine(stats[0], stats[1], stats[2], 1)
    mine_lp = chosen - (peak + jnp.log(total))

    local_ids = tensor_id * rows_local + jnp.arange(rows_local, dtype=jnp.int32)
    keep_token = local_ids % SCORE_LEN < score_len[local_ids // SCORE_LEN]
    return jnp.where(keep_token[None, :], mine_lp, 0.0)


def solution(mesh):
    in_specs = (
        P(None, "group", "tensor"),
        P(None, "group", None, "tensor"),
        P(None, "group", None, None, "tensor"),
        P(),
        P(),
        P("group"),
        P(None, "tensor", None),
        P(None, ("group", "tensor"), None),
        P(),
        P(),
        P(None, None, ("group", "tensor")),
        P(),
    )
    out_specs = P(None, ("group", "tensor"))
    return jax.shard_map(
        per_device, mesh=mesh, in_specs=in_specs, out_specs=out_specs, check_vma=False
    )
```

time: 522 us -> 331 us (0.63)
  blocking collectives: 148 us -> 16.4 us
  waiting for transfers between devices: 221 us -> 193 us
  local copies, waits for them, and re-layouts: 65 us -> 38.5 us
  other arithmetic: 30.6 us -> 18.5 us
  starting transfers between devices: 12.5 us -> 22.2 us
    pmax x1 -> x0, blocking collectives: 74.5 us -> none  [per_device(): row_peak = lax.pmax(jnp.max(logits, axis=2), ('group', 'tensor'))]
    psum x1 -> x0, blocking collectives: 73.8 us -> none  [per_device(): lax.psum((jnp.sum(jnp.exp(logits - row_peak[..., None]), axis=2), jnp.whe...]
    unnamed x3 -> x1, waiting for transfers between devices: 62.5 us -> 0.02 us
    all_to_all x1, waiting for transfers between devices: 38.9 us -> 65.1 us  [per_device(): lax.all_to_all(outgoing, 'group', split_axis=1, concat_axis=1, tiled=True)]
    another operation x4 -> x2, other arithmetic: 19.7 us -> 1.02 us  [the longest x1 1.01 us: per_device(): jnp.stack([local_peak, local_total, local_chosen])]
    scatter x3 -> x0, local copies, waits for them, and re-layouts: 18 us -> none  [the longest x2 11.8 us: per_device(): outgoing = outgoing.at[:, my_dest * capacity + my_position].set(kv_pages)]
    all_to_all x0 -> x1, blocking collectives: none -> 16.4 us  [per_device(): lax.all_to_all(partial.reshape(shards, rows_local, 2, width), 'tensor', 0...]
    all_to_all x0 -> x2, waiting for transfers between devices: none -> 13.1 us  [the longest x1 9.06 us: per_device(): lax.all_to_all(jnp.stack([peak, total, chosen]), 'group', 2, 2, tiled=True)]
  transfers between devices with their start and end apart: 3 -> 4, of which waited for: 3 -> 4; matrix products, arithmetic and copies ran while one was open for 6% -> 2% of each run, Pallas kernels for 0% -> 0%
where the time goes in v1:
time: 331 us; the launch traced here: 330 us
  waiting for transfers between devices  193 us (58%)
  local copies, waits for them, and re-layouts  38.5 us (12%)
  matrix products  28.1 us (8%)
  starting transfers between devices  22.2 us (7%)
  other arithmetic  18.5 us (6%)
  blocking collectives  16.4 us (5%)
  between operations  13.7 us (4%)
    all_gather x1, waiting for transfers between devices, per_device(): everyone = lax.all_gather(normed, ('group', 'tensor'), axis=1, tiled=True)  114 us
    all_to_all x1, waiting for transfers between devices, per_device(): lax.all_to_all(outgoing, 'group', split_axis=1, concat_axis=1, tiled=True)  65.1 us
    dot_general x1, matrix products, per_device(): jnp.einsum('mnd,mdv->mnv', everyone, vocab, preferred_element_type=jnp.fl...  23.1 us
    all_to_all x1, blocking collectives, per_device(): lax.all_to_all(partial.reshape(shards, rows_local, 2, width), 'tensor', 0...  16.4 us
    all_to_all x1, starting transfers between devices, per_device(): lax.all_to_all(outgoing, 'group', split_axis=1, concat_axis=1, tiled=True)  12.3 us
    slice x2, local copies, waits for them, and re-layouts, per_device(): incoming[:, :, :, 1].reshape(2, buffer * page_len, head_local, HEAD_DIM)  11.5 us
    gather x1, local copies, waits for them, and re-layouts, per_device(): outgoing = jnp.take(kv_pages, send_from, axis=1)  10.7 us
    all_to_all x1, waiting for transfers between devices, per_device(): lax.all_to_all(jnp.stack([peak, total, chosen]), 'group', 2, 2, tiled=True)  9.06 us
  transfers between devices with their start and end apart: 4, of which 4 were waited for; matrix products, arithmetic and copies ran while one was open for 2% of the time, Pallas kernels for 0%

profile of v1, /device:TPU:1, one launch (start us, length us, event | category | flops | bytes accessed | tf_op | source)
XLA Modules:
  0.0 330.0 jit_solution(15946534215800585845)
XLA Ops:
  6.5 0.9 dynamic-slice_bitcast_fusion
  7.4 0.2 convert_reduce_fusion.2
  7.6 0.8 multiply_add_fusion
  8.4 0.1 select_reduce_fusion.3
  8.5 10.7 %gather_fusion.1 = bf16[96,2,16,2,256]{4,3,2,1,0:T(2,128)(2,1)} fusion(bf16[2,48,16,2,256]{4,3,2,1,0:T(2,128)(2,1)} %param.14, s32[1024]{0:T(1024)S(1)} %pad_clamp_fusion), kind=kCustom, calls=%fused_computation.1 | custom fusion | bytes 6291840 | tf_op jit(solution)/shard_map/jit(_take)/gather | solution.py:67
  19.2 6.4 %fusion.2 = bf16[2,96,16,2,256]{4,3,2,0,1:T(2,128)(2,1)} fusion(bf16[96,2,16,2,256]{4,3,2,1,0:T(2,128)(2,1)} %gather_fusion.1, pred[96]{0:T(512)(128)(4,1)S(1)} %compare_and_fusion.1), kind=kLoop, calls=%fused_computation.8 | loop fusion | flops 1572864 | bytes 6291552 | tf_op jit(solution)/shard_map/jit(_take)/select_n | solution.py:67
  25.6 12.3 %all-to-all-start = ((bf16[2,96,16,2,256]{4,3,2,0,1:T(2,128)(2,1)}), bf16[2,96,16,2,256]{4,3,2,0,1:T(2,128)(2,1)}, u32[]{:S(2)}, u32[]{:S(2)}) async-start(bf16[2,96,16,2,256]{4,3,2,0,1:T(2,128)(2,1)} %fusion.2), calls=%async_computation | async-start | bytes 6291456 | tf_op jit(solution)/shard_map/all_to_all | solution.py:68
  37.9 0.2 all-gather.2.cloned.1.call-start
  38.2 0.1 eq.156
  38.3 0.6 convert_reduce_fusion
  39.0 0.3 select_reduce_fusion.2
  39.3 0.3 convert_reduce_fusion.1
  39.6 0.1 iota_add_fusion
  39.7 0.1 add.233
  39.8 0.2 fusion.29
  40.1 0.1 eq.160
  40.2 0.1 dynamic_slice.10
  40.2 0.1 fusion.58
  40.4 0.6 fusion.74
  41.0 1.2 fusion.67
  42.2 0.3 slice_reduce_fusion
  42.5 0.1 compare_and_fusion
  42.7 0.2 fusion.76
  42.9 0.1 broadcast_compare_fusion
  43.0 0.1 subtract_convert_fusion
  43.1 0.1 broadcast_multiply_fusion
  43.2 65.1 %all-to-all-done = bf16[2,96,16,2,256]{4,3,2,0,1:T(2,128)(2,1)} async-done(((bf16[2,96,16,2,256]{4,3,2,0,1:T(2,128)(2,1)}), bf16[2,96,16,2,256]{4,3,2,0,1:T(2,128)(2,1)}, u32[]{:S(2)}, u32[]{:S(2)}) %all-to-all-start) | async-done | bytes 3145760 | tf_op jit(solution)/shard_map/all_to_all | solution.py:68
  108.2 9.8 %fusion.73 = (bf16[2,96,16,1,256]{4,3,2,0,1:T(2,128)(2,1)}, bf16[2,96,16,1,256]{4,3,2,0,1:T(2,128)(2,1)S(1)}) fusion(bf16[2,96,16,2,256]{4,3,2,0,1:T(2,128)(2,1)} %all-to-all-done), kind=kLoop, calls=%fused_computation.145 | loop fusion | bytes 6291456 | tf_op jit(solution)/shard_map/slice | solution.py:117
  118.1 1.6 copy.71
  119.7 3.5 %reshape_squeeze.13 = bf16[2,1536,2,128]{3,2,1,0:T(2,128)(2,1)} reshape(bf16[2,96,16,1,256]{4,2,1,0,3:T(8,128)(2,1)} %copy.71) | data formatting | bytes 3145728 | tf_op jit(solution)/shard_map/reshape;squeeze | solution.py:116
  123.2 2.3 fusion.75
  125.5 0.3 fusion.26
  125.9 0.2 convolution_bitcast_fusion.1
  126.1 1.6 copy.70
  127.7 3.5 %reshape_squeeze.12 = bf16[2,1536,2,128]{3,2,1,0:T(2,128)(2,1)} reshape(bf16[2,96,16,1,256]{4,2,1,0,3:T(8,128)(2,1)} %copy.70) | data formatting | bytes 3145728 | tf_op jit(solution)/shard_map/reshape;squeeze | solution.py:117
  131.2 1.9 fusion.23
  133.2 0.5 convolution_bitcast_fusion
  133.6 0.2 reshape.477
  133.8 16.4 %all_to_all.20 = f32[8,4,2,2048]{3,1,2,0:T(4,128)S(1)} all-to-all(f32[8,4,2,2048]{3,1,2,0:T(4,128)S(1)} %copy.80), channel_id=1, replica_groups=mesh['group'=32,'tensor'=8] {'tensor'}, dimensions={0} | all-to-all | bytes 1048576 | tf_op jit(solution)/shard_map/all_to_all | solution.py:156
  150.2 0.1 reduce_sum.174
  150.3 0.1 fusion.57
  150.4 0.2 multiply_reduce_fusion
  150.6 0.1 add_convert_fusion
  150.7 0.6 copy.81
  151.4 0.6 iota_compare_fusion
  152.0 114.4 %all-gather.2.cloned.1.call-done = bf16[2,1024,2048]{2,0,1:T(2,128)(2,1)} async-done(((bf16[2,4,2048]{2,0,1:T(2,128)(2,1)}), bf16[2,1024,2048]{2,0,1:T(2,128)(2,1)}) %all-gather.2.cloned.1.call-update) | async-done | bytes 8388624 | tf_op jit(solution)/shard_map/all_gather | solution.py:170
  266.4 23.1 %fusion.77 = (f32[2,1024]{1,0:T(2,128)S(1)}, f32[2,1024,768]{1,2,0:T(8,128)}) fusion(bf16[2,2048,768]{2,1,0:T(8,128)(2,1)} %param.22, bf16[2,1024,2048]{2,0,1:T(2,128)(2,1)} %all-gather.2.cloned.1.call-done), kind=kOutput, calls=%fused_computation.149 | convolution fusion | flops 6444021760 | bytes 20979712 | tf_op jit(solution)/shard_map/mnd,mdv->mnv/dot_general | solution.py:171
  289.5 0.3 stack.21
  289.8 3.6 %exponential_reduce_fusion = (f32[2,1024]{1,0:T(2,128)S(1)}, f32[2,1024]{1,0:T(2,128)S(1)}) fusion(f32[2,1024,768]{1,2,0:T(8,128)} %get-tuple-element.20, f32[2,1024]{1,0:T(2,128)S(1)} %get-tuple-element.19, pred[1024,768]{0,1:T(8,128)(4,1)S(1)} %iota_compare_fusion), kind=kLoop, calls=%fused_computation.5 | loop fusion | flops 6287360 | bytes 7102464 | tf_op jit(solution)/shard_map/reduce_sum | solution.py:173
  293.4 0.3 stack.22
  293.7 1.0 stack.23
  294.7 1.0 pad_maximum_fusion
  295.7 0.4 copy.84
  296.1 0.7 reshape.516
  296.8 4.3 %all-to-all-start.2 = ((f32[8,1,768]{2,1,0:T(1,128)}), f32[8,1,768]{2,1,0:T(1,128)S(1)}, u32[]{:S(2)}, u32[]{:S(2)}) async-start(f32[8,1,768]{2,1,0:T(1,128)} %reshape.516), calls=%async_computation.2 | async-start | bytes 49152 | tf_op jit(solution)/shard_map/all_to_all | solution.py:181
  301.1 0.6 gather_fusion
  301.8 4.0 %all-to-all-done.2 = f32[8,1,768]{2,1,0:T(1,128)S(1)} async-done(((f32[8,1,768]{2,1,0:T(1,128)}), f32[8,1,768]{2,1,0:T(1,128)S(1)}, u32[]{:S(2)}, u32[]{:S(2)}) %all-to-all-start.2) | async-done | bytes 24608 | tf_op jit(solution)/shard_map/all_to_all | solution.py:181
  305.8 0.5 broadcast.583
  306.3 0.7 reduce.11
  307.0 0.1 reshape.517
  307.2 0.7 copy.86
  308.0 5.4 %all-to-all-start.3 = ((f32[3,2,32,4]{3,1,0,2:T(2,128)}), f32[3,2,32,4]{3,1,0,2:T(2,128)S(1)}, u32[]{:S(2)}, u32[]{:S(2)}) async-start(f32[3,2,32,4]{3,1,0,2:T(2,128)} %copy.86), calls=%async_computation.3 | async-start | bytes 196608 | tf_op jit(solution)/shard_map/all_to_all | solution.py:183
  313.4 9.1 %all-to-all-done.3 = f32[3,2,32,4]{3,1,0,2:T(2,128)S(1)} async-done(((f32[3,2,32,4]{3,1,0,2:T(2,128)}), f32[3,2,32,4]{3,1,0,2:T(2,128)S(1)}, u32[]{:S(2)}, u32[]{:S(2)}) %all-to-all-start.3) | async-done | bytes 3104 | tf_op jit(solution)/shard_map/all_to_all | solution.py:183
  322.6 0.6 subtract_select_fusion
  (54 shorter events, 0.8 us)
Async XLA Ops:
  6.5 126.6 %copy-start = (bf16[2,256,2048]{2,1,0:T(8,128)(2,1)S(1)}, bf16[2,256,2048]{2,1,0:T(8,128)(2,1)}, u32[]{:S(2)}) copy-start(bf16[2,256,2048]{2,1,0:T(8,128)(2,1)} %param.18) | copy-start | bytes 6291460
  25.6 12.5 %copy-start.9 = (s32[1536,1]{0,1:T(1,128)S(1)}, s32[1536,1]{0,1:T(1,128)}, u32[]{:S(2)}) copy-start(s32[1536,1]{0,1:T(1,128)} %param.15) | copy-start | bytes 18436
  25.6 13.4 %copy-start.5 = (s32[1536]{0:T(1024)S(1)}, s32[1536]{0:T(1024)}, u32[]{:S(2)}) copy-start(s32[1536]{0:T(1024)} %param.16) | copy-start | bytes 18436
  25.6 16.6 %copy-start.4 = (bf16[2,32,2,256]{3,2,1,0:T(2,128)(2,1)S(1)}, bf16[2,32,2,256]{3,2,1,0:T(2,128)(2,1)}, u32[]{:S(2)}) copy-start(bf16[2,32,2,256]{3,2,1,0:T(2,128)(2,1)} %param.13) | copy-start | bytes 196612
  25.6 17.1 %copy-start.6 = (bf16[2,32,256]{2,1,0:T(8,128)(2,1)S(1)}, bf16[2,32,256]{2,1,0:T(8,128)(2,1)}, u32[]{:S(2)}) copy-start(bf16[2,32,256]{2,1,0:T(8,128)(2,1)} %param.12) | copy-start | bytes 98308
  25.6 82.6 %all-to-all-start = ((bf16[2,96,16,2,256]{4,3,2,0,1:T(2,128)(2,1)}), bf16[2,96,16,2,256]{4,3,2,0,1:T(2,128)(2,1)}, u32[]{:S(2)}, u32[]{:S(2)}) async-start(bf16[2,96,16,2,256]{4,3,2,0,1:T(2,128)(2,1)} %fusion.2), calls=%async_computation | async-start | bytes 6291456 | tf_op jit(solution)/shard_map/all_to_all | solution.py:68
  37.9 228.5 %all-gather.2.cloned.1.call-start = ((), (), s32[]{:S(2)}) async-start(), calls=%async_computation.4 | async-start | bytes 8421376 | tf_op jit(solution)/shard_map/all_gather | solution.py:170
  123.2 2.9 copy-start.2
  133.1 17.2 %copy-start.3 = (bf16[2,4,2048]{2,1,0:T(4,128)(2,1)S(1)}, bf16[2,4,2048]{2,1,0:T(4,128)(2,1)}, u32[]{:S(2)}) copy-start(bf16[2,4,2048]{2,1,0:T(4,128)(2,1)} %param.19) | copy-start | bytes 98308
  133.1 17.5 %copy-start.7 = (f32[2,2048]{1,0:T(2,128)S(1)}, f32[2,2048]{1,0:T(2,128)}, u32[]{:S(2)}) copy-start(f32[2,2048]{1,0:T(2,128)} %param.21) | copy-start | bytes 49156
  133.1 17.5 %copy-start.8 = (f32[2,2048]{1,0:T(2,128)S(1)}, f32[2,2048]{1,0:T(2,128)}, u32[]{:S(2)}) copy-start(f32[2,2048]{1,0:T(2,128)} %param.20) | copy-start | bytes 49156
  133.1 18.3 %copy-start.10 = (s32[1024]{0:T(1024)S(1)}, s32[1024]{0:T(1024)}, u32[]{:S(2)}) copy-start(s32[1024]{0:T(1024)} %param.23) | copy-start | bytes 12292
  293.4 7.7 %copy-start.1 = (s32[2]{0:T(128)S(1)}, s32[2]{0:T(128)}, u32[]{:S(2)}) copy-start(s32[2]{0:T(128)} %param.17) | copy-start | bytes 28
  296.8 9.0 %all-to-all-start.2 = ((f32[8,1,768]{2,1,0:T(1,128)}), f32[8,1,768]{2,1,0:T(1,128)S(1)}, u32[]{:S(2)}, u32[]{:S(2)}) async-start(f32[8,1,768]{2,1,0:T(1,128)} %reshape.516), calls=%async_computation.2 | async-start | bytes 49152 | tf_op jit(solution)/shard_map/all_to_all | solution.py:181
  308.0 14.5 %all-to-all-start.3 = ((f32[3,2,32,4]{3,1,0,2:T(2,128)}), f32[3,2,32,4]{3,1,0,2:T(2,128)S(1)}, u32[]{:S(2)}, u32[]{:S(2)}) async-start(f32[3,2,32,4]{3,1,0,2:T(2,128)} %copy.86), calls=%async_computation.3 | async-start | bytes 196608 | tf_op jit(solution)/shard_map/all_to_all | solution.py:183
Sparse Core Ops, SparseCore 0:
  151.5 114.8 all-gather.1

commit v2 on v1

--- a/solution.py
+++ b/solution.py
@@ -62,10 +62,11 @@
     )
     out_slot = my_dest * capacity + my_position
     slots = jnp.arange(buffer, dtype=jnp.int32)
-    send_hot = out_slot[None, :] == slots[:, None]
-    send_from = jnp.sum(jnp.where(send_hot, local[None, :], 0), axis=1)
-    outgoing = jnp.take(kv_pages, send_from, axis=1)
-    incoming = lax.all_to_all(outgoing, "group", split_axis=1, concat_axis=1, tiled=True)
+    send_hot = (out_slot[None, :] == slots[:, None]).astype(kv_pages.dtype)
+    outgoing = jnp.einsum(
+        "sp,mpjcx->cmsjx", send_hot, kv_pages, preferred_element_type=jnp.float32
+    ).astype(kv_pages.dtype)
+    incoming = lax.all_to_all(outgoing, "group", split_axis=2, concat_axis=2, tiled=True)
 
     pages = jnp.arange(page_total, dtype=jnp.int32)
     mine = destination == group_id
@@ -113,8 +114,8 @@
     own_scores = jnp.where(own_allowed, own_scores, NEGATIVE)
     own_top = jnp.max(own_scores, -1)
 
-    key_data = incoming[:, :, :, 0].reshape(2, buffer * page_len, head_local, HEAD_DIM)
-    values = incoming[:, :, :, 1].reshape(2, buffer * page_len, head_local, HEAD_DIM)
+    key_data = incoming[0].reshape(2, buffer * page_len, head_local, HEAD_DIM)
+    values = incoming[1].reshape(2, buffer * page_len, head_local, HEAD_DIM)
     key_request = jnp.repeat(jnp.where(is_valid, slot_request, -1), page_len)
     key_position = (
         slot_rank[:, None] * page_len + jnp.arange(page_len, dtype=jnp.int32)[None, :]
@@ -167,17 +168,66 @@
 
     voc_local = vocab.shape[2]
     offset = (group_id * shards + tensor_id) * voc_local
-    everyone = lax.all_gather(normed, ("group", "tensor"), axis=1, tiled=True)
-    logits = jnp.einsum("mnd,mdv->mnv", everyone, vocab, preferred_element_type=jnp.float32)
-    local_peak = jnp.max(logits, axis=2)
-    local_total = jnp.sum(jnp.exp(logits - local_peak[..., None]), axis=2)
-    wanted = targets - offset
-    hit = jnp.arange(voc_local, dtype=jnp.int32)[None, None, :] == wanted[None, :, None]
-    local_chosen = jnp.sum(jnp.where(hit, logits, 0.0), axis=2)
-
-    stats = jnp.stack([local_peak, local_total, local_chosen]).reshape(
-        3, 2, groups, shards, rows_local
-    )
+    side = tensor_id % 2
+    y_size = 4
+    z_size = groups // y_size
+    z_id = group_id // y_size
+    y_id = group_id % y_size
+    block = lax.all_gather(normed, "tensor", axis=0, tiled=False)
+    block = lax.dynamic_index_in_dim(block, side, 1, keepdims=False)
+
+    def y_shift(step):
+        return [(z * y_size + y, z * y_size + (y + step) % y_size)
+                for z in range(z_size) for y in range(y_size)]
+
+    def z_shift(step):
+        return [(z * y_size + y, ((z + step) % z_size) * y_size + y)
+                for z in range(z_size) for y in range(y_size)]
+
+    block = jnp.stack([block] + [lax.ppermute(block, "group", y_shift(k)) for k in range(1, y_size)])
+    forward, backward = block, block
+    chunks = [block]
+    z_from = [0]
+    for k in range(1, z_size // 2 + 1):
+        forward = lax.ppermute(forward, "group", z_shift(1))
+        chunks.append(forward)
+        z_from.append(k)
+        if k < z_size // 2:
+            backward = lax.ppermute(backward, "group", z_shift(z_size - 1))
+            chunks.append(backward)
+            z_from.append(z_size - k)
+    own_model = jnp.stack(chunks)
+    other_model = lax.ppermute(
+        own_model, "tensor", [(t, t ^ 1) for t in range(shards)]
+    )
+    z_from = jnp.array(z_from, dtype=jnp.int32)
+    y_from = jnp.arange(y_size, dtype=jnp.int32)
+    source_group = (
+        ((z_id - z_from[:, None]) % z_size) * y_size + (y_id - y_from[None, :]) % y_size
+    ).reshape(-1)
+    token_rows = shards * rows_local
+    wanted = (targets.reshape(groups, token_rows)[source_group] - offset).reshape(-1)
+    lanes = jnp.arange(voc_local, dtype=jnp.int32)
+
+    def local_stats(rows, weights):
+        logits = jnp.dot(rows.reshape(-1, width), weights, preferred_element_type=jnp.float32)
+        peak = jnp.max(logits, axis=1)
+        total = jnp.sum(jnp.exp(logits - peak[:, None]), axis=1)
+        chosen = jnp.sum(jnp.where(lanes[None, :] == wanted[:, None], logits, 0.0), axis=1)
+        return jnp.stack([peak, total, chosen])
+
+    own_stats = local_stats(own_model, lax.dynamic_index_in_dim(vocab, side, 0, keepdims=False))
+    other_stats = local_stats(
+        other_model, lax.dynamic_index_in_dim(vocab, 1 - side, 0, keepdims=False)
+    )
+    stats = jnp.where(
+        side == 0, jnp.stack([own_stats, other_stats], 1), jnp.stack([other_stats, own_stats], 1)
+    ).reshape(3, 2, groups, token_rows)
+    inverse = jnp.zeros((groups,), jnp.int32).at[source_group].set(
+        jnp.arange(groups, dtype=jnp.int32)
+    )
+    stats = jnp.take(stats, inverse, axis=2).reshape(3, 2, groups, shards, rows_local)
+
     stats = lax.all_to_all(stats, "tensor", 3, 3, tiled=True)
     peak, total, chosen = lse_combine(stats[0], stats[1], stats[2], 2)
     stats = lax.all_to_all(jnp.stack([peak, total, chosen]), "group", 2, 2, tiled=True)

time: 331 us -> 281 us (0.85)
  waiting for transfers between devices: 193 us -> 132 us
  starting transfers between devices: 22.2 us -> 41.3 us
  local copies, waits for them, and re-layouts: 38.5 us -> 57.1 us
  between operations: 13.7 us -> 0.45 us
  other arithmetic: 18.5 us -> 13 us
  matrix products: 28.1 us -> 23 us
    all_gather x1 -> x0, waiting for transfers between devices: 114 us -> none  [per_device(): everyone = lax.all_gather(normed, ('group', 'tensor'), axis=1, tiled=True)]
    ppermute x0 -> x11, waiting for transfers between devices: none -> 44.5 us  [the longest x4 35.7 us: per_device(): forward = lax.ppermute(forward, 'group', z_shift(1))]
    all_to_all x1 -> x0, blocking collectives: 16.4 us -> none  [per_device(): lax.all_to_all(partial.reshape(shards, rows_local, 2, width), 'tensor', 0...]
    ppermute x0 -> x11, starting transfers between devices: none -> 15 us  [the longest x3 5.06 us: per_device(): backward = lax.ppermute(backward, 'group', z_shift(z_size - 1))]
    reshape x0 -> x3, local copies, waits for them, and re-layouts: none -> 13.9 us  [the longest x2 13.8 us: local_stats(): rows.reshape(-1, width)]
    all_gather x0 -> x1, blocking collectives: none -> 13.7 us  [per_device(): block = lax.all_gather(normed, 'tensor', axis=0, tiled=False)]
    gather x1 -> x3, local copies, waits for them, and re-layouts: 10.7 us -> 1.36 us  [the longest x2 0.79 us: per_device(): jnp.take(stats, inverse, axis=2).reshape(3, 2, groups, shards, rows_local)]
    all_to_all x1 -> x2, waiting for transfers between devices: 65.1 us -> 74.2 us  [the longest x1 64.7 us: per_device(): lax.all_to_all(outgoing, 'group', split_axis=2, concat_axis=2, tiled=True)]
  transfers between devices with their start and end apart: 4 -> 15, of which waited for: 4 -> 11; matrix products, arithmetic and copies ran while one was open for 2% -> 11% of each run, Pallas kernels for 0% -> 0%
where the time goes in v2:
time: 281 us; the launch traced here: 280 us
  waiting for transfers between devices  132 us (47%)
  local copies, waits for them, and re-layouts  57.1 us (20%)
  starting transfers between devices  41.3 us (15%)
  matrix products  23 us (8%)
  blocking collectives  13.7 us (5%)
  other arithmetic  13 us (5%)
    all_to_all x1, waiting for transfers between devices, per_device(): lax.all_to_all(outgoing, 'group', split_axis=2, concat_axis=2, tiled=True)  64.7 us
    ppermute x4, waiting for transfers between devices, per_device(): forward = lax.ppermute(forward, 'group', z_shift(1))  35.7 us
    dot_general x2, matrix products, local_stats(): jnp.dot(rows.reshape(-1, width), weights, preferred_element_type=jnp.floa...  16.6 us
    reshape x2, local copies, waits for them, and re-layouts, local_stats(): rows.reshape(-1, width)  13.8 us
    all_gather x1, blocking collectives, per_device(): block = lax.all_gather(normed, 'tensor', axis=0, tiled=False)  13.7 us
    all_to_all x1, starting transfers between devices, per_device(): lax.all_to_all(outgoing, 'group', split_axis=2, concat_axis=2, tiled=True)  12.3 us
    slice x2, local copies, waits for them, and re-layouts, per_device(): values = incoming[1].reshape(2, buffer * page_len, head_local, HEAD_DIM)  11.5 us
    all_to_all x1, waiting for transfers between devices, per_device(): lax.all_to_all(partial.reshape(shards, rows_local, 2, width), 'tensor', 0...  9.48 us
  transfers between devices with their start and end apart: 15, of which 11 were waited for; matrix products, arithmetic and copies ran while one was open for 11% of the time, Pallas kernels for 0%

profile of v2, /device:TPU:1, one launch (start us, length us, event | category | flops | bytes accessed | tf_op | source)
XLA Modules:
  0.0 280.3 jit_solution(6000665489049031114)
XLA Ops:
  0.0 0.9 fusion.76
  1.1 0.8 multiply_add_fusion
  1.8 2.8 convert_bitcast_fusion
  4.6 4.9 %copy.67 = bf16[2,2,96,16,256]{4,0,3,1,2:T(2,128)(2,1)} copy(bf16[2,2,96,16,256]{4,2,0,3,1:T(8,128)(2,1)S(1)} %convert_bitcast_fusion) | data formatting | bytes 6291456 | tf_op jit(solution)/shard_map/convert_element_type | solution.py:68
  9.5 12.3 %all-to-all-start = ((bf16[2,2,96,16,256]{4,0,3,1,2:T(2,128)(2,1)}), bf16[2,2,96,16,256]{4,0,3,1,2:T(2,128)(2,1)}, u32[]{:S(2)}, u32[]{:S(2)}) async-start(bf16[2,2,96,16,256]{4,0,3,1,2:T(2,128)(2,1)} %copy.67), calls=%async_computation | async-start | bytes 6291456 | tf_op jit(solution)/shard_map/all_to_all | solution.py:69
  22.2 0.6 convert_reduce_fusion
  24.1 0.7 scatter_custom_fusion
  25.0 0.6 fusion.89
  25.5 1.2 and_select_fusion.2
  27.8 64.7 %all-to-all-done = bf16[2,2,96,16,256]{4,0,3,1,2:T(2,128)(2,1)} async-done(((bf16[2,2,96,16,256]{4,0,3,1,2:T(2,128)(2,1)}), bf16[2,2,96,16,256]{4,0,3,1,2:T(2,128)(2,1)}, u32[]{:S(2)}, u32[]{:S(2)}) %all-to-all-start) | async-done | bytes 3145760 | tf_op jit(solution)/shard_map/all_to_all | solution.py:69
  92.4 9.8 %fusion.88 = (bf16[1,2,96,16,256]{4,0,3,1,2:T(2,128)(2,1)S(1)}, bf16[1,2,96,16,256]{4,0,3,1,2:T(2,128)(2,1)}) fusion(bf16[2,2,96,16,256]{4,0,3,1,2:T(2,128)(2,1)} %all-to-all-done), kind=kLoop, calls=%fused_computation.188 | loop fusion | bytes 6291456 | tf_op jit(solution)/shard_map/slice | solution.py:118
  102.3 1.7 copy.68
  103.9 3.5 %reshape_squeeze.12 = bf16[2,1536,2,128]{3,2,1,0:T(2,128)(2,1)} reshape(bf16[1,2,96,16,256]{4,3,2,1,0:T(8,128)(2,1)} %copy.68) | data formatting | bytes 3145728 | tf_op jit(solution)/shard_map/reshape;squeeze | solution.py:118
  107.4 3.5 %copy.69 = bf16[1,2,96,16,256]{4,3,2,1,0:T(8,128)(2,1)} copy(bf16[1,2,96,16,256]{4,0,3,1,2:T(2,128)(2,1)} %get-tuple-element.16) | data formatting | bytes 3145728 | tf_op jit(solution)/shard_map/slice | solution.py:117
  110.9 3.5 %reshape_squeeze.13 = bf16[2,1536,2,128]{3,2,1,0:T(2,128)(2,1)} reshape(bf16[1,2,96,16,256]{4,3,2,1,0:T(8,128)(2,1)} %copy.69) | data formatting | bytes 3145728 | tf_op jit(solution)/shard_map/reshape;squeeze | solution.py:117
  114.4 2.3 fusion.90
  117.2 0.5 fusion.27
  117.8 0.5 convolution_bitcast_fusion
  118.5 0.8 copy.78
  119.3 6.9 %all-to-all-start.1 = ((f32[8,4,2,2048]{3,1,2,0:T(4,128)}), f32[8,4,2,2048]{3,1,2,0:T(4,128)S(1)}, u32[]{:S(2)}, u32[]{:S(2)}) async-start(f32[8,4,2,2048]{3,1,2,0:T(4,128)} %copy.78), calls=%async_computation.1 | async-start | bytes 1048576 | tf_op jit(solution)/shard_map/all_to_all | solution.py:157
  126.2 9.5 %all-to-all-done.1 = f32[8,4,2,2048]{3,1,2,0:T(4,128)S(1)} async-done(((f32[8,4,2,2048]{3,1,2,0:T(4,128)}), f32[8,4,2,2048]{3,1,2,0:T(4,128)S(1)}, u32[]{:S(2)}, u32[]{:S(2)}) %all-to-all-start.1) | async-done | bytes 524320 | tf_op jit(solution)/shard_map/all_to_all | solution.py:157
  136.2 13.7 %all-gather = bf16[16,4,2048]{2,1,0:T(4,128)(2,1)S(1)} all-gather(bf16[2,4,2048]{2,1,0:T(4,128)(2,1)S(1)} %add_convert_fusion), channel_id=2, replica_groups=mesh['group'=32,'tensor'=8] {'tensor'}, dimensions={0}, use_global_device_ids=true | all-gather | bytes 294912 | tf_op jit(solution)/shard_map/all_gather | solution.py:176
  150.0 1.8 collective-permute-start.2
  151.8 0.6 collective-permute-start.1
  152.4 0.4 collective-permute-start
  152.8 2.3 collective-permute-done.2
  155.0 2.9 %collective-permute-done.1 = bf16[8,4,2048]{2,1,0:T(4,128)(2,1)S(1)} collective-permute-done((bf16[8,4,2048]{2,1,0:T(4,128)(2,1)S(1)}, bf16[8,4,2048]{2,1,0:T(4,128)(2,1)S(1)}, u32[]{:S(2)}, u32[]{:S(2)}) %collective-permute-start.1) | collective-permute-done | bytes 131104 | tf_op jit(solution)/shard_map/ppermute | solution.py:187
  157.9 3.6 %collective-permute-done = bf16[8,4,2048]{2,1,0:T(4,128)(2,1)S(1)} collective-permute-done((bf16[8,4,2048]{2,1,0:T(4,128)(2,1)S(1)}, bf16[8,4,2048]{2,1,0:T(4,128)(2,1)S(1)}, u32[]{:S(2)}, u32[]{:S(2)}) %collective-permute-start) | collective-permute-done | bytes 131104 | tf_op jit(solution)/shard_map/ppermute | solution.py:187
  161.5 0.5 pad_maximum_fusion
  162.0 2.2 collective-permute-start.3
  164.1 0.6 collective-permute-start.4
  164.7 1.1 bitcast_dynamic-update-slice_fusion.7
  165.8 10.4 %collective-permute-done.3 = bf16[4,8,4,2048]{3,2,1,0:T(4,128)(2,1)S(1)} collective-permute-done((bf16[4,8,4,2048]{3,2,1,0:T(4,128)(2,1)S(1)}, bf16[4,8,4,2048]{3,2,1,0:T(4,128)(2,1)S(1)}, u32[]{:S(2)}, u32[]{:S(2)}) %collective-permute-start.3) | collective-permute-done | bytes 524320 | tf_op jit(solution)/shard_map/ppermute | solution.py:192
  176.3 0.9 collective-permute-start.5
  177.1 1.8 collective-permute-start.6
  178.9 1.1 bitcast_dynamic-update-slice_fusion.6
  180.0 1.1 bitcast_dynamic-update-slice_fusion.5
  181.1 8.5 %collective-permute-done.5 = bf16[4,8,4,2048]{3,2,1,0:T(4,128)(2,1)S(1)} collective-permute-done((bf16[4,8,4,2048]{3,2,1,0:T(4,128)(2,1)S(1)}, bf16[4,8,4,2048]{3,2,1,0:T(4,128)(2,1)S(1)}, u32[]{:S(2)}, u32[]{:S(2)}) %collective-permute-start.5) | collective-permute-done | bytes 524320 | tf_op jit(solution)/shard_map/ppermute | solution.py:192
  189.6 2.7 collective-permute-start.8
  192.2 1.1 bitcast_dynamic-update-slice_fusion.4
  193.3 1.1 bitcast_dynamic-update-slice_fusion.3
  194.4 7.6 %collective-permute-done.7 = bf16[4,8,4,2048]{3,2,1,0:T(4,128)(2,1)S(1)} collective-permute-done((bf16[4,8,4,2048]{3,2,1,0:T(4,128)(2,1)S(1)}, bf16[4,8,4,2048]{3,2,1,0:T(4,128)(2,1)S(1)}, u32[]{:S(2)}, u32[]{:S(2)}) %collective-permute-start.7) | collective-permute-done | bytes 524320 | tf_op jit(solution)/shard_map/ppermute | solution.py:192
  201.9 1.1 bitcast_dynamic-update-slice_fusion.2
  203.0 1.0 bitcast_dynamic-update-slice_fusion.1
  204.0 9.3 %collective-permute-done.9 = bf16[4,8,4,2048]{3,2,1,0:T(4,128)(2,1)S(1)} collective-permute-done((bf16[4,8,4,2048]{3,2,1,0:T(4,128)(2,1)S(1)}, bf16[4,8,4,2048]{3,2,1,0:T(4,128)(2,1)S(1)}, u32[]{:S(2)}, u32[]{:S(2)}) %collective-permute-start.9) | collective-permute-done | bytes 524320 | tf_op jit(solution)/shard_map/ppermute | solution.py:192
  213.4 1.1 bitcast_dynamic-update-slice_fusion
  214.4 4.1 %collective-permute-start.10 = (bf16[8,4,8,4,2048]{4,3,2,1,0:T(4,128)(2,1)}, bf16[8,4,8,4,2048]{4,3,2,1,0:T(4,128)(2,1)}, u32[]{:S(2)}, u32[]{:S(2)}) collective-permute-start(bf16[8,4,8,4,2048]{4,3,2,1,0:T(4,128)(2,1)} %bitcast_dynamic-update-slice_fusion), channel_id=1, source_target_pairs={{0,1},{1,0},{2,3},{3,2},{4,5},{5,4},{6,7},{7,6},{8,9},{9,8},{10,11... | collective-permute-start | bytes 12582920 | tf_op jit(solution)/shard_map/ppermute | solution.py:200
  218.6 0.6 gather_fusion.1
  219.3 6.9 %reshape.538 = bf16[1024,2048]{1,0:T(8,128)(2,1)} reshape(bf16[8,4,8,4,2048]{4,3,2,1,0:T(4,128)(2,1)} %bitcast_dynamic-update-slice_fusion) | data formatting | bytes 8388608 | tf_op jit(solution)/shard_map/reshape | solution.py:213
  226.2 8.3 %fusion.93 = (f32[1024]{0:T(1024)S(1)}, f32[1024,768]{0,1:T(8,128)}) fusion(bf16[1024,2048]{1,0:T(8,128)(2,1)} %reshape.538, bf16[2,2048,768]{2,1,0:T(8,128)(2,1)} %param.23, s32[]{:T(128)S(6)} %select_n.237), kind=kOutput, calls=%fused_computation.193 | convolution fusion | flops 3222010880 | bytes 10489860 | tf_op jit(solution)/shard_map/dot_general | solution.py:213
  234.6 6.9 %reshape.540 = bf16[1024,2048]{1,0:T(8,128)(2,1)} reshape(bf16[8,4,8,4,2048]{4,3,2,1,0:T(4,128)(2,1)} %collective-permute-done.10) | data formatting | bytes 8388608 | tf_op jit(solution)/shard_map/reshape | solution.py:213
  241.5 8.3 %fusion.92 = (f32[1024]{0:T(1024)S(1)}, f32[1024,768]{0,1:T(8,128)}) fusion(bf16[1024,2048]{1,0:T(8,128)(2,1)} %reshape.540, bf16[2,2048,768]{2,1,0:T(8,128)(2,1)} %param.23, s32[]{:T(128)S(6)} %select_n.239), kind=kOutput, calls=%fused_computation.192 | convolution fusion | flops 3222010880 | bytes 10489860 | tf_op jit(solution)/shard_map/dot_general | solution.py:213
  249.9 4.3 %select_reduce_fusion.1 = (f32[1024]{0:T(1024)S(1)}, f32[1024]{0:T(1024)S(1)}, f32[1024]{0:T(1024)S(1)}, f32[1024]{0:T(1024)S(1)}) fusion(f32[1024,768]{0,1:T(8,128)} %get-tuple-element.28, s32[1024]{0:T(1024)S(1)} %sub.192, f32[1024]{0:T(1024)S(1)} %get-tuple-element.27, f32[1024,768]{0,1:T(8,128)} %get-tuple-element.26, f32[1024]{0:T(1024)S(1)} %get-tuple-element.25), kind=kLoop, calls=%fused_computation.11 | loop fusion | flops 7073792 | bytes 6320128 | tf_op jit(solution)/shard_map/reduce_sum | solution.py:216
  254.9 0.7 gather_fusion.2
  255.7 0.7 reshape.600
  256.5 3.3 %all-to-all-start.2 = ((f32[8,1,768]{2,1,0:T(1,128)}), f32[8,1,768]{2,1,0:T(1,128)S(1)}, u32[]{:S(2)}, u32[]{:S(2)}) async-start(f32[8,1,768]{2,1,0:T(1,128)} %reshape.600), calls=%async_computation.2 | async-start | bytes 49152 | tf_op jit(solution)/shard_map/all_to_all | solution.py:231
  259.8 0.6 gather_fusion
  260.4 4.0 %all-to-all-done.2 = f32[8,1,768]{2,1,0:T(1,128)S(1)} async-done(((f32[8,1,768]{2,1,0:T(1,128)}), f32[8,1,768]{2,1,0:T(1,128)S(1)}, u32[]{:S(2)}, u32[]{:S(2)}) %all-to-all-start.2) | async-done | bytes 24608 | tf_op jit(solution)/shard_map/all_to_all | solution.py:231
  264.4 0.5 broadcast.657
  264.9 0.7 reduce.11
  265.8 0.7 copy.82
  266.6 3.9 %all-to-all-start.3 = ((f32[3,2,32,4]{3,1,0,2:T(2,128)}), f32[3,2,32,4]{3,1,0,2:T(2,128)S(1)}, u32[]{:S(2)}, u32[]{:S(2)}) async-start(f32[3,2,32,4]{3,1,0,2:T(2,128)} %copy.82), calls=%async_computation.3 | async-start | bytes 196608 | tf_op jit(solution)/shard_map/all_to_all | solution.py:233
  270.5 9.1 %all-to-all-done.3 = f32[3,2,32,4]{3,1,0,2:T(2,128)S(1)} async-done(((f32[3,2,32,4]{3,1,0,2:T(2,128)}), f32[3,2,32,4]{3,1,0,2:T(2,128)S(1)}, u32[]{:S(2)}, u32[]{:S(2)}) %all-to-all-start.3) | async-done | bytes 3104 | tf_op jit(solution)/shard_map/all_to_all | solution.py:233
  279.7 0.6 subtract_select_fusion
  (107 shorter events, 5.6 us)
Async XLA Ops:
  0.0 117.8 %copy-start = (bf16[2,256,2048]{2,1,0:T(8,128)(2,1)S(1)}, bf16[2,256,2048]{2,1,0:T(8,128)(2,1)}, u32[]{:S(2)}) copy-start(bf16[2,256,2048]{2,1,0:T(8,128)(2,1)} %param.19) | copy-start | bytes 6291460
  9.5 12.4 %copy-start.11 = (s32[8]{0:T(128)S(1)}, s32[8]{0:T(128)}, u32[]{:S(2)}) copy-start(s32[8]{0:T(128)} %constant.199) | copy-start | bytes 100
  9.5 12.5 %copy-start.9 = (s32[1536,1]{0,1:T(1,128)S(1)}, s32[1536,1]{0,1:T(1,128)}, u32[]{:S(2)}) copy-start(s32[1536,1]{0,1:T(1,128)} %param.16) | copy-start | bytes 18436
  9.5 13.4 %copy-start.5 = (s32[1536]{0:T(1024)S(1)}, s32[1536]{0:T(1024)}, u32[]{:S(2)}) copy-start(s32[1536]{0:T(1024)} %param.17) | copy-start | bytes 18436
  9.5 17.3 %copy-start.4 = (bf16[2,32,2,256]{3,2,1,0:T(2,128)(2,1)S(1)}, bf16[2,32,2,256]{3,2,1,0:T(2,128)(2,1)}, u32[]{:S(2)}) copy-start(bf16[2,32,2,256]{3,2,1,0:T(2,128)(2,1)} %param.14) | copy-start | bytes 196612
  9.5 17.8 %copy-start.6 = (bf16[2,32,256]{2,1,0:T(8,128)(2,1)S(1)}, bf16[2,32,256]{2,1,0:T(8,128)(2,1)}, u32[]{:S(2)}) copy-start(bf16[2,32,256]{2,1,0:T(8,128)(2,1)} %param.13) | copy-start | bytes 98308
  9.5 82.9 %all-to-all-start = ((bf16[2,2,96,16,256]{4,0,3,1,2:T(2,128)(2,1)}), bf16[2,2,96,16,256]{4,0,3,1,2:T(2,128)(2,1)}, u32[]{:S(2)}, u32[]{:S(2)}) async-start(bf16[2,2,96,16,256]{4,0,3,1,2:T(2,128)(2,1)} %copy.67), calls=%async_computation | async-start | bytes 6291456 | tf_op jit(solution)/shard_map/all_to_all | solution.py:69
  114.4 2.8 %copy-start.2 = (bf16[2,1536,2,128]{3,2,1,0:T(2,128)(2,1)S(1)}, bf16[2,1536,2,128]{3,2,1,0:T(2,128)(2,1)}, u32[]{:S(2)}) copy-start(bf16[2,1536,2,128]{3,2,1,0:T(2,128)(2,1)} %reshape_squeeze.12) | copy-start | bytes 4718596
  117.8 18.0 %copy-start.3 = (bf16[2,4,2048]{2,1,0:T(4,128)(2,1)S(1)}, bf16[2,4,2048]{2,1,0:T(4,128)(2,1)}, u32[]{:S(2)}) copy-start(bf16[2,4,2048]{2,1,0:T(4,128)(2,1)} %param.20) | copy-start | bytes 98308
  117.8 18.3 %copy-start.7 = (f32[2,2048]{1,0:T(2,128)S(1)}, f32[2,2048]{1,0:T(2,128)}, u32[]{:S(2)}) copy-start(f32[2,2048]{1,0:T(2,128)} %param.22) | copy-start | bytes 49156
  117.8 18.3 %copy-start.8 = (f32[2,2048]{1,0:T(2,128)S(1)}, f32[2,2048]{1,0:T(2,128)}, u32[]{:S(2)}) copy-start(f32[2,2048]{1,0:T(2,128)} %param.21) | copy-start | bytes 49156
  119.3 16.4 %all-to-all-start.1 = ((f32[8,4,2,2048]{3,1,2,0:T(4,128)}), f32[8,4,2,2048]{3,1,2,0:T(4,128)S(1)}, u32[]{:S(2)}, u32[]{:S(2)}) async-start(f32[8,4,2,2048]{3,1,2,0:T(4,128)} %copy.78), calls=%async_computation.1 | async-start | bytes 1048576 | tf_op jit(solution)/shard_map/all_to_all | solution.py:157
  150.0 5.0 %collective-permute-start.2 = (bf16[8,4,2048]{2,1,0:T(4,128)(2,1)S(1)}, bf16[8,4,2048]{2,1,0:T(4,128)(2,1)S(1)}, u32[]{:S(2)}, u32[]{:S(2)}) collective-permute-start(bf16[8,4,2048]{2,1,0:T(4,128)(2,1)S(1)} %get-tuple-element.18), channel_id=1, source_target_pairs={{0,24},{8,0},{16,8},{24,16},{32,56},{40,32},{48,40},{56,48},{64,88... | collective-permute-start | bytes 393224 | tf_op jit(solution)/shard_map/ppermute | solution.py:187
  151.8 6.1 %collective-permute-start.1 = (bf16[8,4,2048]{2,1,0:T(4,128)(2,1)S(1)}, bf16[8,4,2048]{2,1,0:T(4,128)(2,1)S(1)}, u32[]{:S(2)}, u32[]{:S(2)}) collective-permute-start(bf16[8,4,2048]{2,1,0:T(4,128)(2,1)S(1)} %get-tuple-element.18), channel_id=1, source_target_pairs={{0,16},{8,24},{16,0},{24,8},{32,48},{40,56},{48,32},{56,40},{64,80... | collective-permute-start | bytes 393224 | tf_op jit(solution)/shard_map/ppermute | solution.py:187
  152.4 9.1 %collective-permute-start = (bf16[8,4,2048]{2,1,0:T(4,128)(2,1)S(1)}, bf16[8,4,2048]{2,1,0:T(4,128)(2,1)S(1)}, u32[]{:S(2)}, u32[]{:S(2)}) collective-permute-start(bf16[8,4,2048]{2,1,0:T(4,128)(2,1)S(1)} %get-tuple-element.18), channel_id=1, source_target_pairs={{0,8},{8,16},{16,24},{24,0},{32,40},{40,48},{48,56},{56,32},{64,72... | collective-permute-start | bytes 393224 | tf_op jit(solution)/shard_map/ppermute | solution.py:187
  162.0 14.3 %collective-permute-start.3 = (bf16[4,8,4,2048]{3,2,1,0:T(4,128)(2,1)S(1)}, bf16[4,8,4,2048]{3,2,1,0:T(4,128)(2,1)S(1)}, u32[]{:S(2)}, u32[]{:S(2)}) collective-permute-start(bf16[4,8,4,2048]{3,2,1,0:T(4,128)(2,1)S(1)} %pad_maximum_fusion), channel_id=1, source_target_pairs={{0,32},{8,40},{16,48},{24,56},{32,64},{40,72},{48,80},{56,88},{64,... | collective-permute-start | bytes 1572872 | tf_op jit(solution)/shard_map/ppermute | solution.py:192
  164.1 13.0 %collective-permute-start.4 = (bf16[4,8,4,2048]{3,2,1,0:T(4,128)(2,1)S(1)}, bf16[4,8,4,2048]{3,2,1,0:T(4,128)(2,1)S(1)}, u32[]{:S(2)}, u32[]{:S(2)}) collective-permute-start(bf16[4,8,4,2048]{3,2,1,0:T(4,128)(2,1)S(1)} %pad_maximum_fusion), channel_id=1, source_target_pairs={{0,224},{8,232},{16,240},{24,248},{32,0},{40,8},{48,16},{56,24},{6... | collective-permute-start | bytes 1572872 | tf_op jit(solution)/shard_map/ppermute | solution.py:196
  176.3 13.3 %collective-permute-start.5 = (bf16[4,8,4,2048]{3,2,1,0:T(4,128)(2,1)S(1)}, bf16[4,8,4,2048]{3,2,1,0:T(4,128)(2,1)S(1)}, u32[]{:S(2)}, u32[]{:S(2)}) collective-permute-start(bf16[4,8,4,2048]{3,2,1,0:T(4,128)(2,1)S(1)} %collective-permute-done.3), channel_id=1, source_target_pairs={{0,32},{8,40},{16,48},{24,56},{32,64},{40,72},{48,80},{56,88},{64,... | collective-permute-start | bytes 1572872 | tf_op jit(solution)/shard_map/ppermute | solution.py:192
  177.1 12.4 %collective-permute-start.6 = (bf16[4,8,4,2048]{3,2,1,0:T(4,128)(2,1)S(1)}, bf16[4,8,4,2048]{3,2,1,0:T(4,128)(2,1)S(1)}, u32[]{:S(2)}, u32[]{:S(2)}) collective-permute-start(bf16[4,8,4,2048]{3,2,1,0:T(4,128)(2,1)S(1)} %collective-permute-done.4), channel_id=1, source_target_pairs={{0,224},{8,232},{16,240},{24,248},{32,0},{40,8},{48,16},{56,24},{6... | collective-permute-start | bytes 1572872 | tf_op jit(solution)/shard_map/ppermute | solution.py:196
  180.0 38.5 %copy-start.10 = (s32[1024]{0:T(1024)S(1)}, s32[1024]{0:T(1024)}, u32[]{:S(2)}) copy-start(s32[1024]{0:T(1024)} %param.24) | copy-start | bytes 12292
  189.5 12.4 %collective-permute-start.7 = (bf16[4,8,4,2048]{3,2,1,0:T(4,128)(2,1)S(1)}, bf16[4,8,4,2048]{3,2,1,0:T(4,128)(2,1)S(1)}, u32[]{:S(2)}, u32[]{:S(2)}) collective-permute-start(bf16[4,8,4,2048]{3,2,1,0:T(4,128)(2,1)S(1)} %collective-permute-done.5), channel_id=1, source_target_pairs={{0,32},{8,40},{16,48},{24,56},{32,64},{40,72},{48,80},{56,88},{64,... | collective-permute-start | bytes 1572872 | tf_op jit(solution)/shard_map/ppermute | solution.py:192
  189.6 13.4 %collective-permute-start.8 = (bf16[4,8,4,2048]{3,2,1,0:T(4,128)(2,1)S(1)}, bf16[4,8,4,2048]{3,2,1,0:T(4,128)(2,1)S(1)}, u32[]{:S(2)}, u32[]{:S(2)}) collective-permute-start(bf16[4,8,4,2048]{3,2,1,0:T(4,128)(2,1)S(1)} %collective-permute-done.6), channel_id=1, source_target_pairs={{0,224},{8,232},{16,240},{24,248},{32,0},{40,8},{48,16},{56,24},{6... | collective-permute-start | bytes 1572872 | tf_op jit(solution)/shard_map/ppermute | solution.py:196
  201.9 11.4 %collective-permute-start.9 = (bf16[4,8,4,2048]{3,2,1,0:T(4,128)(2,1)S(1)}, bf16[4,8,4,2048]{3,2,1,0:T(4,128)(2,1)S(1)}, u32[]{:S(2)}, u32[]{:S(2)}) collective-permute-start(bf16[4,8,4,2048]{3,2,1,0:T(4,128)(2,1)S(1)} %collective-permute-done.7), channel_id=1, source_target_pairs={{0,32},{8,40},{16,48},{24,56},{32,64},{40,72},{48,80},{56,88},{64,... | collective-permute-start | bytes 1572872 | tf_op jit(solution)/shard_map/ppermute | solution.py:192
  214.4 20.2 %collective-permute-start.10 = (bf16[8,4,8,4,2048]{4,3,2,1,0:T(4,128)(2,1)}, bf16[8,4,8,4,2048]{4,3,2,1,0:T(4,128)(2,1)}, u32[]{:S(2)}, u32[]{:S(2)}) collective-permute-start(bf16[8,4,8,4,2048]{4,3,2,1,0:T(4,128)(2,1)} %bitcast_dynamic-update-slice_fusion), channel_id=1, source_target_pairs={{0,1},{1,0},{2,3},{3,2},{4,5},{5,4},{6,7},{7,6},{8,9},{9,8},{10,11... | collective-permute-start | bytes 12582920 | tf_op jit(solution)/shard_map/ppermute | solution.py:200
  249.9 9.8 %copy-start.1 = (s32[2]{0:T(128)S(1)}, s32[2]{0:T(128)}, u32[]{:S(2)}) copy-start(s32[2]{0:T(128)} %param.18) | copy-start | bytes 28
  256.5 7.9 %all-to-all-start.2 = ((f32[8,1,768]{2,1,0:T(1,128)}), f32[8,1,768]{2,1,0:T(1,128)S(1)}, u32[]{:S(2)}, u32[]{:S(2)}) async-start(f32[8,1,768]{2,1,0:T(1,128)} %reshape.600), calls=%async_computation.2 | async-start | bytes 49152 | tf_op jit(solution)/shard_map/all_to_all | solution.py:231
  266.6 13.0 %all-to-all-start.3 = ((f32[3,2,32,4]{3,1,0,2:T(2,128)}), f32[3,2,32,4]{3,1,0,2:T(2,128)S(1)}, u32[]{:S(2)}, u32[]{:S(2)}) async-start(f32[3,2,32,4]{3,1,0,2:T(2,128)} %copy.82), calls=%async_computation.3 | async-start | bytes 196608 | tf_op jit(solution)/shard_map/all_to_all | solution.py:233

commit v3 on v2

--- a/solution.py
+++ b/solution.py
@@ -95,62 +95,54 @@
 
     slopes = lax.dynamic_slice_in_dim(alibi_slopes(HEADS), tensor_id * head_local, head_local)
     score_scale = 1.0 / math.sqrt(HEAD_DIM)
-    queries = query.reshape(2, tok_grp, head_local, HEAD_DIM)
-    own_keys = self_kv[:, :, 0].reshape(2, tok_grp, head_local, HEAD_DIM)
-    own_values = self_kv[:, :, 1].reshape(2, tok_grp, head_local, HEAD_DIM)
     token_ids = jnp.arange(tok_grp, dtype=jnp.int32)
     token_request = token_ids // SCORE_LEN
     token_step = token_ids % SCORE_LEN
     own_distance = (token_step[:, None] - token_step[None, :]).astype(jnp.float32)
-    own_scores = (
-        jnp.einsum("mthd,mshd->mhts", queries, own_keys, preferred_element_type=jnp.float32)
-        * score_scale
-    )
-    own_scores = own_scores - slopes[None, :, None, None] * own_distance[None, None]
     own_allowed = (
         (token_request[:, None] == token_request[None, :])
         & (token_step[None, :] <= token_step[:, None])
-    )[None, None]
-    own_scores = jnp.where(own_allowed, own_scores, NEGATIVE)
-    own_top = jnp.max(own_scores, -1)
-
-    key_data = incoming[0].reshape(2, buffer * page_len, head_local, HEAD_DIM)
-    values = incoming[1].reshape(2, buffer * page_len, head_local, HEAD_DIM)
+    )[None]
     key_request = jnp.repeat(jnp.where(is_valid, slot_request, -1), page_len)
     key_position = (
         slot_rank[:, None] * page_len + jnp.arange(page_len, dtype=jnp.int32)[None, :]
     ).reshape(-1)
     context = totals[token_request] * page_len
     distance = ((context + token_step)[:, None] - key_position[None, :]).astype(jnp.float32)
-    scores = (
-        jnp.einsum("mthd,mkhd->mhtk", queries, key_data, preferred_element_type=jnp.float32)
-        * score_scale
-    )
-    scores = scores - slopes[None, :, None, None] * distance[None, None]
-    allowed = (key_request[None, :] == token_request[:, None])[None, None]
-    scores = jnp.where(allowed, scores, NEGATIVE)
-    row_top = jnp.maximum(jnp.max(scores, -1), own_top)
-    exp_terms = jnp.where(allowed, jnp.exp(scores - row_top[..., None]), 0.0)
-    denominator = jnp.sum(exp_terms, -1)
-    numerator = jnp.einsum(
-        "mhtk,mkhd->mthd",
-        exp_terms.astype(jnp.bfloat16),
-        values,
-        preferred_element_type=jnp.float32,
-    )
-    own_terms = jnp.where(own_allowed, jnp.exp(own_scores - row_top[..., None]), 0.0)
-    denominator = denominator + jnp.sum(own_terms, -1)
-    numerator = numerator + jnp.einsum(
-        "mhts,mshd->mthd",
-        own_terms.astype(jnp.bfloat16),
-        own_values,
-        preferred_element_type=jnp.float32,
-    )
-    attended = (
-        (numerator / jnp.transpose(denominator, (0, 2, 1))[..., None])
-        .reshape(2, tok_grp, flat_width)
-        .astype(jnp.bfloat16)
-    )
+    allowed = (key_request[None, :] == token_request[:, None])[None]
+    page_keys = incoming[0].reshape(2, buffer * page_len, flat_width)
+    page_values = incoming[1].reshape(2, buffer * page_len, flat_width)
+    heads_out = []
+    for h in range(head_local):
+        lanes_h = slice(h * HEAD_DIM, (h + 1) * HEAD_DIM)
+        q = query[:, :, lanes_h]
+        own_k = self_kv[:, :, 0, lanes_h]
+        own_v = self_kv[:, :, 1, lanes_h]
+        slope = slopes[h]
+        own_scores = (
+            jnp.einsum("mtd,msd->mts", q, own_k, preferred_element_type=jnp.float32) * score_scale
+        )
+        own_scores = own_scores - slope * own_distance[None]
+        own_scores = jnp.where(own_allowed, own_scores, NEGATIVE)
+        scores = (
+            jnp.einsum("mtd,mkd->mtk", q, page_keys[:, :, lanes_h],
+                       preferred_element_type=jnp.float32) * score_scale
+        )
+        scores = scores - slope * distance[None]
+        scores = jnp.where(allowed, scores, NEGATIVE)
+        row_top = jnp.maximum(jnp.max(scores, -1), jnp.max(own_scores, -1))
+        exp_terms = jnp.where(allowed, jnp.exp(scores - row_top[..., None]), 0.0)
+        own_terms = jnp.where(own_allowed, jnp.exp(own_scores - row_top[..., None]), 0.0)
+        denominator = jnp.sum(exp_terms, -1) + jnp.sum(own_terms, -1)
+        numerator = jnp.einsum(
+            "mtk,mkd->mtd", exp_terms.astype(jnp.bfloat16), page_values[:, :, lanes_h],
+            preferred_element_type=jnp.float32,
+        ) + jnp.einsum(
+            "mts,msd->mtd", own_terms.astype(jnp.bfloat16), own_v,
+            preferred_element_type=jnp.float32,
+        )
+        heads_out.append(numerator / denominator[..., None])
+    attended = jnp.concatenate(heads_out, axis=-1).astype(jnp.bfloat16)
 
     rows_local = tok_grp // shards
     partial = jnp.einsum("mtk,mkd->tmd", attended, out_proj, preferred_element_type=jnp.float32)
@@ -169,12 +161,21 @@
     voc_local = vocab.shape[2]
     offset = (group_id * shards + tensor_id) * voc_local
     side = tensor_id % 2
+    x_size = shards // 2
+    x_id = tensor_id // 2
     y_size = 4
     z_size = groups // y_size
     z_id = group_id // y_size
     y_id = group_id % y_size
-    block = lax.all_gather(normed, "tensor", axis=0, tiled=False)
-    block = lax.dynamic_index_in_dim(block, side, 1, keepdims=False)
+    swap = [(t, t ^ 1) for t in range(shards)]
+    kept = lax.dynamic_index_in_dim(normed, side, 0, keepdims=False)
+    given = lax.ppermute(lax.dynamic_index_in_dim(normed, 1 - side, 0, keepdims=False), "tensor", swap)
+    block = jnp.where(
+        side == 0, jnp.concatenate([kept, given], 0), jnp.concatenate([given, kept], 0)
+    )
+
+    def x_shift(step):
+        return [(t, (t + 2 * step) % shards) for t in range(shards)]
 
     def y_shift(step):
         return [(z * y_size + y, z * y_size + (y + step) % y_size)
@@ -184,7 +185,12 @@
         return [(z * y_size + y, ((z + step) % z_size) * y_size + y)
                 for z in range(z_size) for y in range(y_size)]
 
-    block = jnp.stack([block] + [lax.ppermute(block, "group", y_shift(k)) for k in range(1, y_size)])
+    block = jnp.concatenate(
+        [block] + [lax.ppermute(block, "tensor", x_shift(k)) for k in range(1, x_size)], 0
+    )
+    block = jnp.concatenate(
+        [block] + [lax.ppermute(block, "group", y_shift(k)) for k in range(1, y_size)], 0
+    )
     forward, backward = block, block
     chunks = [block]
     z_from = [0]
@@ -196,21 +202,22 @@
             backward = lax.ppermute(backward, "group", z_shift(z_size - 1))
             chunks.append(backward)
             z_from.append(z_size - k)
-    own_model = jnp.stack(chunks)
-    other_model = lax.ppermute(
-        own_model, "tensor", [(t, t ^ 1) for t in range(shards)]
-    )
+    own_model = jnp.concatenate(chunks, 0)
+    other_model = lax.ppermute(own_model, "tensor", swap)
     z_from = jnp.array(z_from, dtype=jnp.int32)
     y_from = jnp.arange(y_size, dtype=jnp.int32)
     source_group = (
         ((z_id - z_from[:, None]) % z_size) * y_size + (y_id - y_from[None, :]) % y_size
     ).reshape(-1)
-    token_rows = shards * rows_local
-    wanted = (targets.reshape(groups, token_rows)[source_group] - offset).reshape(-1)
+    x_from = (x_id - jnp.arange(x_size, dtype=jnp.int32)) % x_size
+    pair_rows = 2 * rows_local
+    wanted = (
+        targets.reshape(groups, x_size, pair_rows)[source_group[:, None], x_from[None, :]] - offset
+    ).reshape(-1)
     lanes = jnp.arange(voc_local, dtype=jnp.int32)
 
     def local_stats(rows, weights):
-        logits = jnp.dot(rows.reshape(-1, width), weights, preferred_element_type=jnp.float32)
+        logits = jnp.dot(rows, weights, preferred_element_type=jnp.float32)
         peak = jnp.max(logits, axis=1)
         total = jnp.sum(jnp.exp(logits - peak[:, None]), axis=1)
         chosen = jnp.sum(jnp.where(lanes[None, :] == wanted[:, None], logits, 0.0), axis=1)
@@ -222,11 +229,13 @@
     )
     stats = jnp.where(
         side == 0, jnp.stack([own_stats, other_stats], 1), jnp.stack([other_stats, own_stats], 1)
-    ).reshape(3, 2, groups, token_rows)
-    inverse = jnp.zeros((groups,), jnp.int32).at[source_group].set(
+    ).reshape(3, 2, groups, x_size, pair_rows)
+    group_at = jnp.zeros((groups,), jnp.int32).at[source_group].set(
         jnp.arange(groups, dtype=jnp.int32)
     )
-    stats = jnp.take(stats, inverse, axis=2).reshape(3, 2, groups, shards, rows_local)
+    x_at = (x_id - jnp.arange(x_size, dtype=jnp.int32)) % x_size
+    stats = jnp.take(jnp.take(stats, group_at, axis=2), x_at, axis=3)
+    stats = stats.reshape(3, 2, groups, shards, rows_local)
 
     stats = lax.all_to_all(stats, "tensor", 3, 3, tiled=True)
     peak, total, chosen = lse_combine(stats[0], stats[1], stats[2], 2)

time: 281 us -> 245 us (0.87)
  local copies, waits for them, and re-layouts: 57.1 us -> 36.9 us
  blocking collectives: 13.7 us -> 0 us
  waiting for transfers between devices: 132 us -> 119 us
  starting transfers between devices: 41.3 us -> 52.3 us
    reshape x3 -> x1, local copies, waits for them, and re-layouts: 13.9 us -> 0.12 us  [per_device(): targets.reshape(groups, x_size, pair_rows)]
    all_gather x1 -> x0, blocking collectives: 13.7 us -> none  [per_device(): block = lax.all_gather(normed, 'tensor', axis=0, tiled=False)]
    ppermute x3, waiting for transfers between devices: 8.72 us -> 0.82 us  [per_device(): lax.ppermute(block, 'group', y_shift(k))]
    another operation x4 -> x2, local copies, waits for them, and re-layouts: 8.15 us -> 0.42 us  [the longest x1 0.21 us: per_device(): jnp.stack([other_stats, own_stats], 1)]
    ppermute x1 -> x5, starting transfers between devices: 4.1 us -> 10.7 us  [the longest x1 6.69 us: per_device(): other_model = lax.ppermute(own_model, 'tensor', swap)]
    slice x4 -> x3, local copies, waits for them, and re-layouts: 15.2 us -> 9.13 us  [the longest x1 8.45 us: per_device(): page_keys = incoming[0].reshape(2, buffer * page_len, flat_width)]
    ppermute x4, waiting for transfers between devices: 35.7 us -> 29.8 us  [per_device(): forward = lax.ppermute(forward, 'group', z_shift(1))]
    unnamed x36 -> x38, local copies, waits for them, and re-layouts: 7.3 us -> 10.7 us
  transfers between devices with their start and end apart: 15 -> 19, of which waited for: 11 -> 13; matrix products, arithmetic and copies ran while one was open for 11% -> 12% of each run, Pallas kernels for 0% -> 0%
where the time goes in v3:
time: 245 us; the launch traced here: 244 us
  waiting for transfers between devices  119 us (49%)
  starting transfers between devices  52.3 us (21%)
  local copies, waits for them, and re-layouts  36.9 us (15%)
  matrix products  22.2 us (9%)
  other arithmetic  13.9 us (6%)
    all_to_all x1, waiting for transfers between devices, per_device(): lax.all_to_all(outgoing, 'group', split_axis=2, concat_axis=2, tiled=True)  62.8 us
    ppermute x4, waiting for transfers between devices, per_device(): forward = lax.ppermute(forward, 'group', z_shift(1))  29.8 us
    dot_general x2, matrix products, local_stats(): logits = jnp.dot(rows, weights, preferred_element_type=jnp.float32)  16.7 us
    all_to_all x1, starting transfers between devices, per_device(): lax.all_to_all(outgoing, 'group', split_axis=2, concat_axis=2, tiled=True)  12.3 us
    unnamed x38, local copies, waits for them, and re-layouts  10.7 us
    all_to_all x1, waiting for transfers between devices, per_device(): lax.all_to_all(partial.reshape(shards, rows_local, 2, width), 'tensor', 0...  9.48 us
    all_to_all x1, waiting for transfers between devices, per_device(): lax.all_to_all(jnp.stack([peak, total, chosen]), 'group', 2, 2, tiled=True)  9.06 us
    slice x1, local copies, waits for them, and re-layouts, per_device(): page_keys = incoming[0].reshape(2, buffer * page_len, flat_width)  8.45 us
  transfers between devices with their start and end apart: 19, of which 13 were waited for; matrix products, arithmetic and copies ran while one was open for 12% of the time, Pallas kernels for 0%

profile of v3, /device:TPU:1, one launch (start us, length us, event | category | flops | bytes accessed | tf_op | source)
XLA Modules:
  0.0 244.4 jit_solution(1388764680847016044)
XLA Ops:
  0.0 0.9 fusion.85
  1.1 0.8 multiply_add_fusion
  1.8 2.8 %convert_bitcast_fusion = bf16[2,2,96,16,256]{4,2,0,3,1:T(8,128)(2,1)S(1)} fusion(bf16[2,48,16,2,256]{4,3,2,1,0:T(2,128)(2,1)} %param.15, s32[48]{0:T(128)S(1)} %multiply_add_fusion), kind=kOutput, calls=%fused_computation.16 | convolution fusion | flops 152572416 | bytes 4718784 | tf_op jit(solution)/shard_map/sp,mpjcx->cmsjx/dot_general | solution.py:66
  4.6 5.0 %copy.87 = bf16[2,2,96,16,256]{4,0,3,1,2:T(2,128)(2,1)} copy(bf16[2,2,96,16,256]{4,2,0,3,1:T(8,128)(2,1)S(1)} %convert_bitcast_fusion) | data formatting | bytes 6291456 | tf_op jit(solution)/shard_map/convert_element_type | solution.py:68
  9.6 12.3 %all-to-all-start = ((bf16[2,2,96,16,256]{4,0,3,1,2:T(2,128)(2,1)}), bf16[2,2,96,16,256]{4,0,3,1,2:T(2,128)(2,1)}, u32[]{:S(2)}, u32[]{:S(2)}) async-start(bf16[2,2,96,16,256]{4,0,3,1,2:T(2,128)(2,1)} %copy.87), calls=%async_computation | async-start | bytes 6291456 | tf_op jit(solution)/shard_map/all_to_all | solution.py:69
  22.0 0.6 convert_reduce_fusion
  24.1 0.6 fusion.105
  24.7 1.2 fusion.84
  25.9 0.6 fusion.104
  26.6 1.3 convert_multiply_fusion.3
  28.4 1.3 convert_multiply_fusion.1
  29.7 62.8 %all-to-all-done = bf16[2,2,96,16,256]{4,0,3,1,2:T(2,128)(2,1)} async-done(((bf16[2,2,96,16,256]{4,0,3,1,2:T(2,128)(2,1)}), bf16[2,2,96,16,256]{4,0,3,1,2:T(2,128)(2,1)}, u32[]{:S(2)}, u32[]{:S(2)}) %all-to-all-start) | async-done | bytes 3145760 | tf_op jit(solution)/shard_map/all_to_all | solution.py:69
  92.5 8.5 %fusion.102 = (bf16[1,2,96,16,256]{4,0,3,1,2:T(2,128)(2,1)S(1)}, bf16[1,2,96,16,256]{4,0,3,1,2:T(2,128)(2,1)S(1)}) fusion(bf16[2,2,96,16,256]{4,0,3,1,2:T(2,128)(2,1)} %all-to-all-done), kind=kLoop, calls=%fused_computation.240 | loop fusion | bytes 6291456 | tf_op jit(solution)/shard_map/slice | solution.py:113
  104.9 0.8 copy.96
  105.7 6.9 %all-to-all-start.1 = ((f32[8,4,2,2048]{3,1,2,0:T(4,128)}), f32[8,4,2,2048]{3,1,2,0:T(4,128)S(1)}, u32[]{:S(2)}, u32[]{:S(2)}) async-start(f32[8,4,2,2048]{3,1,2,0:T(4,128)} %copy.96), calls=%async_computation.1 | async-start | bytes 1048576 | tf_op jit(solution)/shard_map/all_to_all | solution.py:149
  112.7 9.5 %all-to-all-done.1 = f32[8,4,2,2048]{3,1,2,0:T(4,128)S(1)} async-done(((f32[8,4,2,2048]{3,1,2,0:T(4,128)}), f32[8,4,2,2048]{3,1,2,0:T(4,128)S(1)}, u32[]{:S(2)}, u32[]{:S(2)}) %all-to-all-start.1) | async-done | bytes 524320 | tf_op jit(solution)/shard_map/all_to_all | solution.py:149
  122.7 1.0 collective-permute-start
  123.7 0.8 collective-permute-done
  125.1 1.8 collective-permute-start.2
  126.9 0.7 collective-permute-start.3
  127.6 0.6 constant_dynamic-update-slice_fusion.20
  128.2 0.6 collective-permute-done.1
  128.8 0.6 collective-permute-done.2
  129.4 0.6 collective-permute-done.3
  130.6 2.4 collective-permute-start.5
  132.9 1.0 collective-permute-start.6
  134.0 0.6 constant_dynamic-update-slice_fusion.5
  134.6 0.6 constant_dynamic-update-slice_fusion.4
  135.2 0.6 constant_dynamic-update-slice_fusion.3
  135.8 0.7 constant_dynamic-update-slice_fusion.2
  136.5 0.8 collective-permute-done.5
  137.3 0.7 constant_dynamic-update-slice_fusion.1
  138.0 0.7 constant_dynamic-update-slice_fusion
  138.6 2.1 collective-permute-start.7
  140.7 0.6 collective-permute-start.8
  141.3 9.0 %collective-permute-done.7 = bf16[128,2048]{1,0:T(8,128)(2,1)S(1)} collective-permute-done((bf16[128,2048]{1,0:T(8,128)(2,1)S(1)}, bf16[128,2048]{1,0:T(8,128)(2,1)S(1)}, u32[]{:S(2)}, u32[]{:S(2)}) %collective-permute-start.7) | collective-permute-done | bytes 524320 | tf_op jit(solution)/shard_map/ppermute | solution.py:198
  150.3 0.9 collective-permute-start.9
  151.2 1.8 collective-permute-start.10
  153.0 8.1 %collective-permute-done.9 = bf16[128,2048]{1,0:T(8,128)(2,1)S(1)} collective-permute-done((bf16[128,2048]{1,0:T(8,128)(2,1)S(1)}, bf16[128,2048]{1,0:T(8,128)(2,1)S(1)}, u32[]{:S(2)}, u32[]{:S(2)}) %collective-permute-start.9) | collective-permute-done | bytes 524320 | tf_op jit(solution)/shard_map/ppermute | solution.py:198
  161.6 0.9 constant_dynamic-update-slice_fusion.13
  162.5 0.8 constant_dynamic-update-slice_fusion.12
  163.3 2.2 collective-permute-start.12
  165.5 0.8 constant_dynamic-update-slice_fusion.11
  166.4 5.2 %collective-permute-done.11 = bf16[128,2048]{1,0:T(8,128)(2,1)S(1)} collective-permute-done((bf16[128,2048]{1,0:T(8,128)(2,1)S(1)}, bf16[128,2048]{1,0:T(8,128)(2,1)S(1)}, u32[]{:S(2)}, u32[]{:S(2)}) %collective-permute-start.11) | collective-permute-done | bytes 524320 | tf_op jit(solution)/shard_map/ppermute | solution.py:198
  172.0 0.8 constant_dynamic-update-slice_fusion.10
  172.8 0.9 constant_dynamic-update-slice_fusion.9
  173.7 0.8 constant_dynamic-update-slice_fusion.8
  174.5 7.5 %collective-permute-done.13 = bf16[128,2048]{1,0:T(8,128)(2,1)S(1)} collective-permute-done((bf16[128,2048]{1,0:T(8,128)(2,1)S(1)}, bf16[128,2048]{1,0:T(8,128)(2,1)S(1)}, u32[]{:S(2)}, u32[]{:S(2)}) %collective-permute-start.13) | collective-permute-done | bytes 524320 | tf_op jit(solution)/shard_map/ppermute | solution.py:198
  182.1 0.8 constant_dynamic-update-slice_fusion.7
  182.9 6.7 %collective-permute-start.14 = (bf16[1024,2048]{1,0:T(8,128)(2,1)}, bf16[1024,2048]{1,0:T(8,128)(2,1)}, u32[]{:S(2)}, u32[]{:S(2)}) collective-permute-start(bf16[1024,2048]{1,0:T(8,128)(2,1)} %constant_dynamic-update-slice_fusion.7), channel_id=1, source_target_pairs={{0,1},{1,0},{2,3},{3,2},{4,5},{5,4},{6,7},{7,6},{8,9},{9,8},{10,11... | collective-permute-start | bytes 12582920 | tf_op jit(solution)/shard_map/ppermute | solution.py:206
  190.2 1.0 gather_fusion.1
  191.5 0.9 scatter_custom_fusion
  192.5 8.4 %fusion.110 = (f32[1024]{0:T(1024)S(1)}, f32[1024,768]{0,1:T(8,128)}) fusion(bf16[1024,2048]{1,0:T(8,128)(2,1)} %constant_dynamic-update-slice_fusion.7, bf16[2,2048,768]{2,1,0:T(8,128)(2,1)} %param.23, s32[]{:T(128)S(6)} %select_n.328), kind=kOutput, calls=%fused_computation.248 | convolution fusion | flops 3222010880 | bytes 10489860 | tf_op jit(solution)/shard_map/dot_general | solution.py:220
  201.1 8.3 %fusion.111 = (f32[1024]{0:T(1024)S(1)}, f32[1024,768]{0,1:T(8,128)}) fusion(bf16[1024,2048]{1,0:T(8,128)(2,1)} %collective-permute-done.14, bf16[2,2048,768]{2,1,0:T(8,128)(2,1)} %param.23, s32[]{:T(128)S(6)} %select_n.329), kind=kOutput, calls=%fused_computation.249 | convolution fusion | flops 3222010880 | bytes 10489860 | tf_op jit(solution)/shard_map/dot_general | solution.py:220
  209.5 4.4 %exponential_reduce_fusion.1 = (f32[1024]{0:T(1024)S(1)}, f32[1024]{0:T(1024)S(1)}, f32[1024]{0:T(1024)S(1)}, f32[1024]{0:T(1024)S(1)}) fusion(f32[1024,768]{0,1:T(8,128)} %get-tuple-element.58, f32[1024]{0:T(1024)S(1)} %get-tuple-element.57, s32[1024]{0:T(1024)S(1)} %sub.276, f32[1024,768]{0,1:T(8,128)} %get-tuple-element.60, f32[1024]{0:T(1024)S(1)} %get-tuple-element.59), kind=kLoop, calls=%fused_computation.14 | loop fusion | flops 7073792 | bytes 6320128 | tf_op jit(solution)/shard_map/reduce_sum | solution.py:222
  215.3 0.8 gather_fusion.2
  217.2 0.7 reshape.739
  217.9 3.5 %all-to-all-start.2 = ((f32[8,1,768]{2,1,0:T(1,128)}), f32[8,1,768]{2,1,0:T(1,128)S(1)}, u32[]{:S(2)}, u32[]{:S(2)}) async-start(f32[8,1,768]{2,1,0:T(1,128)} %reshape.739), calls=%async_computation.2 | async-start | bytes 49152 | tf_op jit(solution)/shard_map/all_to_all | solution.py:240
  221.4 0.6 gather_fusion
  222.0 4.0 %all-to-all-done.2 = f32[8,1,768]{2,1,0:T(1,128)S(1)} async-done(((f32[8,1,768]{2,1,0:T(1,128)}), f32[8,1,768]{2,1,0:T(1,128)S(1)}, u32[]{:S(2)}, u32[]{:S(2)}) %all-to-all-start.2) | async-done | bytes 24608 | tf_op jit(solution)/shard_map/all_to_all | solution.py:240
  226.6 0.7 reduce.7
  227.5 0.7 copy.109
  228.2 6.4 %all-to-all-start.3 = ((f32[3,2,32,4]{3,1,0,2:T(2,128)}), f32[3,2,32,4]{3,1,0,2:T(2,128)S(1)}, u32[]{:S(2)}, u32[]{:S(2)}) async-start(f32[3,2,32,4]{3,1,0,2:T(2,128)} %copy.109), calls=%async_computation.3 | async-start | bytes 196608 | tf_op jit(solution)/shard_map/all_to_all | solution.py:242
  234.7 9.1 %all-to-all-done.3 = f32[3,2,32,4]{3,1,0,2:T(2,128)S(1)} async-done(((f32[3,2,32,4]{3,1,0,2:T(2,128)}), f32[3,2,32,4]{3,1,0,2:T(2,128)S(1)}, u32[]{:S(2)}, u32[]{:S(2)}) %all-to-all-start.3) | async-done | bytes 3104 | tf_op jit(solution)/shard_map/all_to_all | solution.py:242
  (135 shorter events, 13.8 us)
Async XLA Ops:
  0.0 104.3 %copy-start = (bf16[2,256,2048]{2,1,0:T(8,128)(2,1)S(1)}, bf16[2,256,2048]{2,1,0:T(8,128)(2,1)}, u32[]{:S(2)}) copy-start(bf16[2,256,2048]{2,1,0:T(8,128)(2,1)} %param.19) | copy-start | bytes 6291460
  9.6 12.3 %copy-start.8 = (s32[1536,1]{0,1:T(1,128)S(1)}, s32[1536,1]{0,1:T(1,128)}, u32[]{:S(2)}) copy-start(s32[1536,1]{0,1:T(1,128)} %param.16) | copy-start | bytes 18436
  9.6 13.2 %copy-start.4 = (s32[1536]{0:T(1024)S(1)}, s32[1536]{0:T(1024)}, u32[]{:S(2)}) copy-start(s32[1536]{0:T(1024)} %param.17) | copy-start | bytes 18436
  9.6 18.3 %copy-start.3 = (bf16[2,32,2,256]{3,2,1,0:T(2,128)(2,1)S(1)}, bf16[2,32,2,256]{3,2,1,0:T(2,128)(2,1)}, u32[]{:S(2)}) copy-start(bf16[2,32,2,256]{3,2,1,0:T(2,128)(2,1)} %param.14) | copy-start | bytes 196612
  9.6 18.4 %copy-start.5 = (bf16[2,32,256]{2,1,0:T(8,128)(2,1)S(1)}, bf16[2,32,256]{2,1,0:T(8,128)(2,1)}, u32[]{:S(2)}) copy-start(bf16[2,32,256]{2,1,0:T(8,128)(2,1)} %param.13) | copy-start | bytes 98308
  9.6 82.9 %all-to-all-start = ((bf16[2,2,96,16,256]{4,0,3,1,2:T(2,128)(2,1)}), bf16[2,2,96,16,256]{4,0,3,1,2:T(2,128)(2,1)}, u32[]{:S(2)}, u32[]{:S(2)}) async-start(bf16[2,2,96,16,256]{4,0,3,1,2:T(2,128)(2,1)} %copy.87), calls=%async_computation | async-start | bytes 6291456 | tf_op jit(solution)/shard_map/all_to_all | solution.py:69
  103.5 18.8 %copy-start.2 = (bf16[2,4,2048]{2,1,0:T(4,128)(2,1)S(1)}, bf16[2,4,2048]{2,1,0:T(4,128)(2,1)}, u32[]{:S(2)}) copy-start(bf16[2,4,2048]{2,1,0:T(4,128)(2,1)} %param.20) | copy-start | bytes 98308
  103.5 19.1 %copy-start.6 = (f32[2,2048]{1,0:T(2,128)S(1)}, f32[2,2048]{1,0:T(2,128)}, u32[]{:S(2)}) copy-start(f32[2,2048]{1,0:T(2,128)} %param.22) | copy-start | bytes 49156
  103.5 19.1 %copy-start.7 = (f32[2,2048]{1,0:T(2,128)S(1)}, f32[2,2048]{1,0:T(2,128)}, u32[]{:S(2)}) copy-start(f32[2,2048]{1,0:T(2,128)} %param.21) | copy-start | bytes 49156
  105.7 16.4 %all-to-all-start.1 = ((f32[8,4,2,2048]{3,1,2,0:T(4,128)}), f32[8,4,2,2048]{3,1,2,0:T(4,128)S(1)}, u32[]{:S(2)}, u32[]{:S(2)}) async-start(f32[8,4,2,2048]{3,1,2,0:T(4,128)} %copy.96), calls=%async_computation.1 | async-start | bytes 1048576 | tf_op jit(solution)/shard_map/all_to_all | solution.py:149
  122.7 1.8 collective-permute-start
  124.5 4.2 %collective-permute-start.1 = (bf16[8,2048]{1,0:T(8,128)(2,1)S(1)}, bf16[8,2048]{1,0:T(8,128)(2,1)S(1)}, u32[]{:S(2)}, u32[]{:S(2)}) collective-permute-start(bf16[8,2048]{1,0:T(8,128)(2,1)S(1)} %get-tuple-element.16), channel_id=1, source_target_pairs={{0,2},{1,3},{2,4},{3,5},{4,6},{5,7},{6,0},{7,1},{8,10},{9,11},{10,... | collective-permute-start | bytes 98312 | tf_op jit(solution)/shard_map/ppermute | solution.py:189
  125.1 4.3 %collective-permute-start.2 = (bf16[8,2048]{1,0:T(8,128)(2,1)S(1)}, bf16[8,2048]{1,0:T(8,128)(2,1)S(1)}, u32[]{:S(2)}, u32[]{:S(2)}) collective-permute-start(bf16[8,2048]{1,0:T(8,128)(2,1)S(1)} %get-tuple-element.16), channel_id=1, source_target_pairs={{0,4},{1,5},{2,6},{3,7},{4,0},{5,1},{6,2},{7,3},{8,12},{9,13},{10,... | collective-permute-start | bytes 98312 | tf_op jit(solution)/shard_map/ppermute | solution.py:189
  126.9 3.1 %collective-permute-start.3 = (bf16[8,2048]{1,0:T(8,128)(2,1)S(1)}, bf16[8,2048]{1,0:T(8,128)(2,1)S(1)}, u32[]{:S(2)}, u32[]{:S(2)}) collective-permute-start(bf16[8,2048]{1,0:T(8,128)(2,1)S(1)} %get-tuple-element.16), channel_id=1, source_target_pairs={{0,6},{1,7},{2,0},{3,1},{4,2},{5,3},{6,4},{7,5},{8,14},{9,15},{10,... | collective-permute-start | bytes 98312 | tf_op jit(solution)/shard_map/ppermute | solution.py:189
  130.0 5.8 %collective-permute-start.4 = (bf16[32,2048]{1,0:T(8,128)(2,1)S(1)}, bf16[32,2048]{1,0:T(8,128)(2,1)S(1)}, u32[]{:S(2)}, u32[]{:S(2)}) collective-permute-start(bf16[32,2048]{1,0:T(8,128)(2,1)S(1)} %pad_maximum_fusion), channel_id=1, source_target_pairs={{0,8},{8,16},{16,24},{24,0},{32,40},{40,48},{48,56},{56,32},{64,72... | collective-permute-start | bytes 393224 | tf_op jit(solution)/shard_map/ppermute | solution.py:192
  130.6 6.7 %collective-permute-start.5 = (bf16[32,2048]{1,0:T(8,128)(2,1)S(1)}, bf16[32,2048]{1,0:T(8,128)(2,1)S(1)}, u32[]{:S(2)}, u32[]{:S(2)}) collective-permute-start(bf16[32,2048]{1,0:T(8,128)(2,1)S(1)} %pad_maximum_fusion), channel_id=1, source_target_pairs={{0,16},{8,24},{16,0},{24,8},{32,48},{40,56},{48,32},{56,40},{64,80... | collective-permute-start | bytes 393224 | tf_op jit(solution)/shard_map/ppermute | solution.py:192
  132.9 5.0 %collective-permute-start.6 = (bf16[32,2048]{1,0:T(8,128)(2,1)S(1)}, bf16[32,2048]{1,0:T(8,128)(2,1)S(1)}, u32[]{:S(2)}, u32[]{:S(2)}) collective-permute-start(bf16[32,2048]{1,0:T(8,128)(2,1)S(1)} %pad_maximum_fusion), channel_id=1, source_target_pairs={{0,24},{8,0},{16,8},{24,16},{32,56},{40,32},{48,40},{56,48},{64,88... | collective-permute-start | bytes 393224 | tf_op jit(solution)/shard_map/ppermute | solution.py:192
  136.5 53.2 %copy-start.10 = (s32[8]{0:T(128)S(1)}, s32[8]{0:T(128)}, u32[]{:S(2)}) copy-start(s32[8]{0:T(128)} %constant.235) | copy-start | bytes 100
  136.5 53.6 %copy-start.9 = (s32[1024]{0:T(1024)S(1)}, s32[1024]{0:T(1024)}, u32[]{:S(2)}) copy-start(s32[1024]{0:T(1024)} %param.24) | copy-start | bytes 12292
  138.6 11.7 %collective-permute-start.7 = (bf16[128,2048]{1,0:T(8,128)(2,1)S(1)}, bf16[128,2048]{1,0:T(8,128)(2,1)S(1)}, u32[]{:S(2)}, u32[]{:S(2)}) collective-permute-start(bf16[128,2048]{1,0:T(8,128)(2,1)S(1)} %get-tuple-element.19), channel_id=1, source_target_pairs={{0,32},{8,40},{16,48},{24,56},{32,64},{40,72},{48,80},{56,88},{64,... | collective-permute-start | bytes 1572872 | tf_op jit(solution)/shard_map/ppermute | solution.py:198
  140.7 10.5 %collective-permute-start.8 = (bf16[128,2048]{1,0:T(8,128)(2,1)S(1)}, bf16[128,2048]{1,0:T(8,128)(2,1)S(1)}, u32[]{:S(2)}, u32[]{:S(2)}) collective-permute-start(bf16[128,2048]{1,0:T(8,128)(2,1)S(1)} %get-tuple-element.19), channel_id=1, source_target_pairs={{0,224},{8,232},{16,240},{24,248},{32,0},{40,8},{48,16},{56,24},{6... | collective-permute-start | bytes 1572872 | tf_op jit(solution)/shard_map/ppermute | solution.py:202
  150.3 10.8 %collective-permute-start.9 = (bf16[128,2048]{1,0:T(8,128)(2,1)S(1)}, bf16[128,2048]{1,0:T(8,128)(2,1)S(1)}, u32[]{:S(2)}, u32[]{:S(2)}) collective-permute-start(bf16[128,2048]{1,0:T(8,128)(2,1)S(1)} %collective-permute-done.7), channel_id=1, source_target_pairs={{0,32},{8,40},{16,48},{24,56},{32,64},{40,72},{48,80},{56,88},{64,... | collective-permute-start | bytes 1572872 | tf_op jit(solution)/shard_map/ppermute | solution.py:198
  151.2 12.1 %collective-permute-start.10 = (bf16[128,2048]{1,0:T(8,128)(2,1)S(1)}, bf16[128,2048]{1,0:T(8,128)(2,1)S(1)}, u32[]{:S(2)}, u32[]{:S(2)}) collective-permute-start(bf16[128,2048]{1,0:T(8,128)(2,1)S(1)} %collective-permute-done.8), channel_id=1, source_target_pairs={{0,224},{8,232},{16,240},{24,248},{32,0},{40,8},{48,16},{56,24},{6... | collective-permute-start | bytes 1572872 | tf_op jit(solution)/shard_map/ppermute | solution.py:202
  161.1 10.4 %collective-permute-start.11 = (bf16[128,2048]{1,0:T(8,128)(2,1)S(1)}, bf16[128,2048]{1,0:T(8,128)(2,1)S(1)}, u32[]{:S(2)}, u32[]{:S(2)}) collective-permute-start(bf16[128,2048]{1,0:T(8,128)(2,1)S(1)} %collective-permute-done.9), channel_id=1, source_target_pairs={{0,32},{8,40},{16,48},{24,56},{32,64},{40,72},{48,80},{56,88},{64,... | collective-permute-start | bytes 1572872 | tf_op jit(solution)/shard_map/ppermute | solution.py:198
  163.3 10.4 %collective-permute-start.12 = (bf16[128,2048]{1,0:T(8,128)(2,1)S(1)}, bf16[128,2048]{1,0:T(8,128)(2,1)S(1)}, u32[]{:S(2)}, u32[]{:S(2)}) collective-permute-start(bf16[128,2048]{1,0:T(8,128)(2,1)S(1)} %collective-permute-done.10), channel_id=1, source_target_pairs={{0,224},{8,232},{16,240},{24,248},{32,0},{40,8},{48,16},{56,24},{6... | collective-permute-start | bytes 1572872 | tf_op jit(solution)/shard_map/ppermute | solution.py:202
  171.5 10.5 %collective-permute-start.13 = (bf16[128,2048]{1,0:T(8,128)(2,1)S(1)}, bf16[128,2048]{1,0:T(8,128)(2,1)S(1)}, u32[]{:S(2)}, u32[]{:S(2)}) collective-permute-start(bf16[128,2048]{1,0:T(8,128)(2,1)S(1)} %collective-permute-done.11), channel_id=1, source_target_pairs={{0,32},{8,40},{16,48},{24,56},{32,64},{40,72},{48,80},{56,88},{64,... | collective-permute-start | bytes 1572872 | tf_op jit(solution)/shard_map/ppermute | solution.py:198
  182.9 18.2 %collective-permute-start.14 = (bf16[1024,2048]{1,0:T(8,128)(2,1)}, bf16[1024,2048]{1,0:T(8,128)(2,1)}, u32[]{:S(2)}, u32[]{:S(2)}) collective-permute-start(bf16[1024,2048]{1,0:T(8,128)(2,1)} %constant_dynamic-update-slice_fusion.7), channel_id=1, source_target_pairs={{0,1},{1,0},{2,3},{3,2},{4,5},{5,4},{6,7},{7,6},{8,9},{9,8},{10,11... | collective-permute-start | bytes 12582920 | tf_op jit(solution)/shard_map/ppermute | solution.py:206
  213.9 7.5 %copy-start.1 = (s32[2]{0:T(128)S(1)}, s32[2]{0:T(128)}, u32[]{:S(2)}) copy-start(s32[2]{0:T(128)} %param.18) | copy-start | bytes 28
  217.9 8.2 %all-to-all-start.2 = ((f32[8,1,768]{2,1,0:T(1,128)}), f32[8,1,768]{2,1,0:T(1,128)S(1)}, u32[]{:S(2)}, u32[]{:S(2)}) async-start(f32[8,1,768]{2,1,0:T(1,128)} %reshape.739), calls=%async_computation.2 | async-start | bytes 49152 | tf_op jit(solution)/shard_map/all_to_all | solution.py:240
  228.2 15.5 %all-to-all-start.3 = ((f32[3,2,32,4]{3,1,0,2:T(2,128)}), f32[3,2,32,4]{3,1,0,2:T(2,128)S(1)}, u32[]{:S(2)}, u32[]{:S(2)}) async-start(f32[3,2,32,4]{3,1,0,2:T(2,128)} %copy.109), calls=%async_computation.3 | async-start | bytes 196608 | tf_op jit(solution)/shard_map/all_to_all | solution.py:242

commit v4 on v3

--- a/solution.py
+++ b/solution.py
@@ -64,9 +64,11 @@
     slots = jnp.arange(buffer, dtype=jnp.int32)
     send_hot = (out_slot[None, :] == slots[:, None]).astype(kv_pages.dtype)
     outgoing = jnp.einsum(
-        "sp,mpjcx->cmsjx", send_hot, kv_pages, preferred_element_type=jnp.float32
+        "sp,mpjcx->scmjx", send_hot, kv_pages, preferred_element_type=jnp.float32
     ).astype(kv_pages.dtype)
-    incoming = lax.all_to_all(outgoing, "group", split_axis=2, concat_axis=2, tiled=True)
+    incoming = lax.all_to_all(
+        outgoing.reshape(buffer, -1, flat_width), "group", split_axis=0, concat_axis=0, tiled=True
+    ).reshape(outgoing.shape)
 
     pages = jnp.arange(page_total, dtype=jnp.int32)
     mine = destination == group_id
@@ -110,8 +112,8 @@
     context = totals[token_request] * page_len
     distance = ((context + token_step)[:, None] - key_position[None, :]).astype(jnp.float32)
     allowed = (key_request[None, :] == token_request[:, None])[None]
-    page_keys = incoming[0].reshape(2, buffer * page_len, flat_width)
-    page_values = incoming[1].reshape(2, buffer * page_len, flat_width)
+    page_keys = incoming[:, 0]
+    page_values = incoming[:, 1]
     heads_out = []
     for h in range(head_local):
         lanes_h = slice(h * HEAD_DIM, (h + 1) * HEAD_DIM)
@@ -125,8 +127,8 @@
         own_scores = own_scores - slope * own_distance[None]
         own_scores = jnp.where(own_allowed, own_scores, NEGATIVE)
         scores = (
-            jnp.einsum("mtd,mkd->mtk", q, page_keys[:, :, lanes_h],
-                       preferred_element_type=jnp.float32) * score_scale
+            jnp.einsum("mtd,smjd->mtsj", q, page_keys[..., lanes_h],
+                       preferred_element_type=jnp.float32).reshape(2, tok_grp, -1) * score_scale
         )
         scores = scores - slope * distance[None]
         scores = jnp.where(allowed, scores, NEGATIVE)
@@ -135,7 +137,9 @@
         own_terms = jnp.where(own_allowed, jnp.exp(own_scores - row_top[..., None]), 0.0)
         denominator = jnp.sum(exp_terms, -1) + jnp.sum(own_terms, -1)
         numerator = jnp.einsum(
-            "mtk,mkd->mtd", exp_terms.astype(jnp.bfloat16), page_values[:, :, lanes_h],
+            "mtsj,smjd->mtd",
+            exp_terms.astype(jnp.bfloat16).reshape(2, tok_grp, buffer, page_len),
+            page_values[..., lanes_h],
             preferred_element_type=jnp.float32,
         ) + jnp.einsum(
             "mts,msd->mtd", own_terms.astype(jnp.bfloat16), own_v,

time: 245 us -> 238 us (0.971)
  local copies, waits for them, and re-layouts: 36.9 us -> 29.1 us
    slice x1, local copies, waits for them, and re-layouts: 8.45 us -> 2.21 us  [per_device(): page_values = incoming[:, 1]]
where the time goes in v4:
time: 238 us
  waiting for transfers between devices  118 us (50%)
  starting transfers between devices  52.1 us (22%)
  local copies, waits for them, and re-layouts  29.1 us (12%)
  matrix products  22.7 us (10%)
  other arithmetic  15.6 us (7%)
    all_to_all x1, waiting for transfers between devices, per_device(): lax.all_to_all(outgoing.reshape(buffer, -1, flat_width), 'group', split_a...  61.7 us
    ppermute x4, waiting for transfers between devices, per_device(): forward = lax.ppermute(forward, 'group', z_shift(1))  29.8 us
    dot_general x2, matrix products, local_stats(): logits = jnp.dot(rows, weights, preferred_element_type=jnp.float32)  16.7 us
    all_to_all x1, starting transfers between devices, per_device(): lax.all_to_all(outgoing.reshape(buffer, -1, flat_width), 'group', split_a...  12.3 us
    unnamed x38, local copies, waits for them, and re-layouts  10.5 us
    all_to_all x1, waiting for transfers between devices, per_device(): lax.all_to_all(partial.reshape(shards, rows_local, 2, width), 'tensor', 0...  9.48 us
    all_to_all x1, waiting for transfers between devices, per_device(): lax.all_to_all(jnp.stack([peak, total, chosen]), 'group', 2, 2, tiled=True)  9.06 us
    all_to_all x1, starting transfers between devices, per_device(): lax.all_to_all(partial.reshape(shards, rows_local, 2, width), 'tensor', 0...  6.93 us
  transfers between devices with their start and end apart: 19, of which 13 were waited for; matrix products, arithmetic and copies ran while one was open for 12% of the time, Pallas kernels for 0%

profile of v4, /device:TPU:1, one launch (start us, length us, event | category | flops | bytes accessed | tf_op | source)
XLA Modules:
  0.0 237.6 jit_solution(15671858124802061431)
XLA Ops:
  0.0 0.9 fusion.81
  1.1 0.8 multiply_add_fusion
  1.8 2.8 %convert_bitcast_fusion = bf16[96,2,2,16,256]{4,0,1,3,2:T(8,128)(2,1)S(1)} fusion(bf16[2,48,16,2,256]{4,3,2,1,0:T(2,128)(2,1)} %param.15, s32[48]{0:T(128)S(1)} %multiply_add_fusion), kind=kOutput, calls=%fused_computation.16 | convolution fusion | flops 152572416 | bytes 4718784 | tf_op jit(solution)/shard_map/sp,mpjcx->scmjx/dot_general | solution.py:66
  4.6 3.5 %copy.88 = bf16[96,2,2,16,256]{4,3,2,1,0:T(8,128)(2,1)} copy(bf16[96,2,2,16,256]{4,0,1,3,2:T(8,128)(2,1)S(1)} %convert_bitcast_fusion) | data formatting | bytes 6291456 | tf_op jit(solution)/shard_map/convert_element_type | solution.py:68
  8.1 12.3 %all-to-all-start = ((bf16[96,64,256]{2,1,0:T(8,128)(2,1)}), bf16[96,64,256]{2,1,0:T(8,128)(2,1)}, u32[]{:S(2)}, u32[]{:S(2)}) async-start(bf16[96,64,256]{2,1,0:T(8,128)(2,1)} %bitcast.149), calls=%async_computation | async-start | bytes 6291456 | tf_op jit(solution)/shard_map/all_to_all | solution.py:69
  20.5 0.6 convert_reduce_fusion
  22.1 1.2 fusion.80
  23.3 0.6 fusion.100
  24.8 1.4 convert_multiply_fusion.3
  26.8 2.4 %convert_multiply_fusion.1 = (f32[32,96,16]{0,2,1:T(8,128)}, f32[32,96,16]{0,2,1:T(8,128)S(1)}) fusion(s32[96,16]{1,0:T(8,128)S(1)} %iota_add_fusion, s32[32]{0:T(128)S(1)} %fusion.80, f32[]{:T(128)} %bitcast.12, f32[]{:T(128)} %bitcast.24), kind=kLoop, calls=%fused_computation.54 | loop fusion | flops 196608 | bytes 399496 | tf_op jit(solution)/shard_map/mul | solution.py:133
  29.2 61.7 %all-to-all-done = bf16[96,64,256]{2,1,0:T(8,128)(2,1)} async-done(((bf16[96,64,256]{2,1,0:T(8,128)(2,1)}), bf16[96,64,256]{2,1,0:T(8,128)(2,1)}, u32[]{:S(2)}, u32[]{:S(2)}) %all-to-all-start) | async-done | bytes 3145760 | tf_op jit(solution)/shard_map/all_to_all | solution.py:69
  91.0 2.2 fusion.98
  93.5 0.8 copy-done.2
  95.9 0.7 fusion.9
  98.3 0.8 copy.97
  99.1 6.9 %all-to-all-start.1 = ((f32[8,4,2,2048]{3,1,2,0:T(4,128)}), f32[8,4,2,2048]{3,1,2,0:T(4,128)S(1)}, u32[]{:S(2)}, u32[]{:S(2)}) async-start(f32[8,4,2,2048]{3,1,2,0:T(4,128)} %copy.97), calls=%async_computation.1 | async-start | bytes 1048576 | tf_op jit(solution)/shard_map/all_to_all | solution.py:153
  106.1 9.5 %all-to-all-done.1 = f32[8,4,2,2048]{3,1,2,0:T(4,128)S(1)} async-done(((f32[8,4,2,2048]{3,1,2,0:T(4,128)}), f32[8,4,2,2048]{3,1,2,0:T(4,128)S(1)}, u32[]{:S(2)}, u32[]{:S(2)}) %all-to-all-start.1) | async-done | bytes 524320 | tf_op jit(solution)/shard_map/all_to_all | solution.py:153
  116.1 1.0 collective-permute-start
  117.0 0.8 collective-permute-done
  118.3 1.8 collective-permute-start.2
  120.1 0.7 collective-permute-start.3
  120.8 0.6 constant_dynamic-update-slice_fusion.20
  121.4 0.6 collective-permute-done.1
  122.6 0.6 collective-permute-done.3
  123.8 2.4 %collective-permute-start.5 = (bf16[32,2048]{1,0:T(8,128)(2,1)S(1)}, bf16[32,2048]{1,0:T(8,128)(2,1)S(1)}, u32[]{:S(2)}, u32[]{:S(2)}) collective-permute-start(bf16[32,2048]{1,0:T(8,128)(2,1)S(1)} %pad_maximum_fusion), channel_id=1, source_target_pairs={{0,16},{8,24},{16,0},{24,8},{32,48},{40,56},{48,32},{56,40},{64,80... | collective-permute-start | bytes 393224 | tf_op jit(solution)/shard_map/ppermute | solution.py:196
  126.1 1.0 collective-permute-start.6
  127.2 0.6 constant_dynamic-update-slice_fusion.5
  127.8 0.6 constant_dynamic-update-slice_fusion.4
  128.4 0.6 constant_dynamic-update-slice_fusion.3
  129.0 0.7 constant_dynamic-update-slice_fusion.2
  129.7 0.8 collective-permute-done.5
  130.5 0.7 constant_dynamic-update-slice_fusion.1
  131.2 0.7 constant_dynamic-update-slice_fusion
  131.8 2.1 collective-permute-start.7
  133.9 0.6 collective-permute-start.8
  134.5 9.0 %collective-permute-done.7 = bf16[128,2048]{1,0:T(8,128)(2,1)S(1)} collective-permute-done((bf16[128,2048]{1,0:T(8,128)(2,1)S(1)}, bf16[128,2048]{1,0:T(8,128)(2,1)S(1)}, u32[]{:S(2)}, u32[]{:S(2)}) %collective-permute-start.7) | collective-permute-done | bytes 524320 | tf_op jit(solution)/shard_map/ppermute | solution.py:202
  143.5 0.9 collective-permute-start.9
  144.4 1.8 collective-permute-start.10
  146.2 8.1 %collective-permute-done.9 = bf16[128,2048]{1,0:T(8,128)(2,1)S(1)} collective-permute-done((bf16[128,2048]{1,0:T(8,128)(2,1)S(1)}, bf16[128,2048]{1,0:T(8,128)(2,1)S(1)}, u32[]{:S(2)}, u32[]{:S(2)}) %collective-permute-start.9) | collective-permute-done | bytes 524320 | tf_op jit(solution)/shard_map/ppermute | solution.py:202
  154.8 0.9 constant_dynamic-update-slice_fusion.13
  155.7 0.8 constant_dynamic-update-slice_fusion.12
  156.5 2.2 collective-permute-start.12
  158.7 0.8 constant_dynamic-update-slice_fusion.11
  159.6 5.1 %collective-permute-done.11 = bf16[128,2048]{1,0:T(8,128)(2,1)S(1)} collective-permute-done((bf16[128,2048]{1,0:T(8,128)(2,1)S(1)}, bf16[128,2048]{1,0:T(8,128)(2,1)S(1)}, u32[]{:S(2)}, u32[]{:S(2)}) %collective-permute-start.11) | collective-permute-done | bytes 524320 | tf_op jit(solution)/shard_map/ppermute | solution.py:202
  165.2 0.8 constant_dynamic-update-slice_fusion.10
  166.0 0.9 constant_dynamic-update-slice_fusion.9
  166.9 0.8 constant_dynamic-update-slice_fusion.8
  167.7 7.5 %collective-permute-done.13 = bf16[128,2048]{1,0:T(8,128)(2,1)S(1)} collective-permute-done((bf16[128,2048]{1,0:T(8,128)(2,1)S(1)}, bf16[128,2048]{1,0:T(8,128)(2,1)S(1)}, u32[]{:S(2)}, u32[]{:S(2)}) %collective-permute-start.13) | collective-permute-done | bytes 524320 | tf_op jit(solution)/shard_map/ppermute | solution.py:202
  175.3 0.8 constant_dynamic-update-slice_fusion.7
  176.1 6.7 %collective-permute-start.14 = (bf16[1024,2048]{1,0:T(8,128)(2,1)}, bf16[1024,2048]{1,0:T(8,128)(2,1)}, u32[]{:S(2)}, u32[]{:S(2)}) collective-permute-start(bf16[1024,2048]{1,0:T(8,128)(2,1)} %constant_dynamic-update-slice_fusion.7), channel_id=1, source_target_pairs={{0,1},{1,0},{2,3},{3,2},{4,5},{5,4},{6,7},{7,6},{8,9},{9,8},{10,11... | collective-permute-start | bytes 12582920 | tf_op jit(solution)/shard_map/ppermute | solution.py:210
  183.4 1.0 gather_fusion.1
  184.7 0.9 scatter_custom_fusion
  185.7 8.4 %fusion.106 = (f32[1024]{0:T(1024)S(1)}, f32[1024,768]{0,1:T(8,128)}) fusion(bf16[1024,2048]{1,0:T(8,128)(2,1)} %constant_dynamic-update-slice_fusion.7, bf16[2,2048,768]{2,1,0:T(8,128)(2,1)} %param.23, s32[]{:T(128)S(6)} %select_n.338), kind=kOutput, calls=%fused_computation.248 | convolution fusion | flops 3222010880 | bytes 10489860 | tf_op jit(solution)/shard_map/dot_general | solution.py:224
  194.3 8.3 %fusion.107 = (f32[1024]{0:T(1024)S(1)}, f32[1024,768]{0,1:T(8,128)}) fusion(bf16[1024,2048]{1,0:T(8,128)(2,1)} %collective-permute-done.14, bf16[2,2048,768]{2,1,0:T(8,128)(2,1)} %param.23, s32[]{:T(128)S(6)} %select_n.339), kind=kOutput, calls=%fused_computation.249 | convolution fusion | flops 3222010880 | bytes 10489860 | tf_op jit(solution)/shard_map/dot_general | solution.py:224
  202.7 4.4 %exponential_reduce_fusion.1 = (f32[1024]{0:T(1024)S(1)}, f32[1024]{0:T(1024)S(1)}, f32[1024]{0:T(1024)S(1)}, f32[1024]{0:T(1024)S(1)}) fusion(f32[1024,768]{0,1:T(8,128)} %get-tuple-element.58, f32[1024]{0:T(1024)S(1)} %get-tuple-element.57, s32[1024]{0:T(1024)S(1)} %sub.286, f32[1024,768]{0,1:T(8,128)} %get-tuple-element.60, f32[1024]{0:T(1024)S(1)} %get-tuple-element.59), kind=kLoop, calls=%fused_computation.14 | loop fusion | flops 7073792 | bytes 6320128 | tf_op jit(solution)/shard_map/reduce_sum | solution.py:226
  208.5 0.8 gather_fusion.2
  210.3 0.7 reshape.788
  211.1 3.5 %all-to-all-start.2 = ((f32[8,1,768]{2,1,0:T(1,128)}), f32[8,1,768]{2,1,0:T(1,128)S(1)}, u32[]{:S(2)}, u32[]{:S(2)}) async-start(f32[8,1,768]{2,1,0:T(1,128)} %reshape.788), calls=%async_computation.2 | async-start | bytes 49152 | tf_op jit(solution)/shard_map/all_to_all | solution.py:244
  214.6 0.6 gather_fusion
  215.2 4.0 %all-to-all-done.2 = f32[8,1,768]{2,1,0:T(1,128)S(1)} async-done(((f32[8,1,768]{2,1,0:T(1,128)}), f32[8,1,768]{2,1,0:T(1,128)S(1)}, u32[]{:S(2)}, u32[]{:S(2)}) %all-to-all-start.2) | async-done | bytes 24608 | tf_op jit(solution)/shard_map/all_to_all | solution.py:244
  219.8 0.7 reduce.11
  220.7 0.7 copy.110
  221.4 6.4 %all-to-all-start.3 = ((f32[3,2,32,4]{3,1,0,2:T(2,128)}), f32[3,2,32,4]{3,1,0,2:T(2,128)S(1)}, u32[]{:S(2)}, u32[]{:S(2)}) async-start(f32[3,2,32,4]{3,1,0,2:T(2,128)} %copy.110), calls=%async_computation.3 | async-start | bytes 196608 | tf_op jit(solution)/shard_map/all_to_all | solution.py:246
  227.8 9.1 %all-to-all-done.3 = f32[3,2,32,4]{3,1,0,2:T(2,128)S(1)} async-done(((f32[3,2,32,4]{3,1,0,2:T(2,128)}), f32[3,2,32,4]{3,1,0,2:T(2,128)S(1)}, u32[]{:S(2)}, u32[]{:S(2)}) %all-to-all-start.3) | async-done | bytes 3104 | tf_op jit(solution)/shard_map/all_to_all | solution.py:246
  (133 shorter events, 14.2 us)
Async XLA Ops:
  0.0 97.6 %copy-start = (bf16[2,256,2048]{2,1,0:T(8,128)(2,1)S(1)}, bf16[2,256,2048]{2,1,0:T(8,128)(2,1)}, u32[]{:S(2)}) copy-start(bf16[2,256,2048]{2,1,0:T(8,128)(2,1)} %param.19) | copy-start | bytes 6291460
  8.1 12.3 %copy-start.9 = (s32[1536,1]{0,1:T(1,128)S(1)}, s32[1536,1]{0,1:T(1,128)}, u32[]{:S(2)}) copy-start(s32[1536,1]{0,1:T(1,128)} %param.16) | copy-start | bytes 18436
  8.1 13.2 %copy-start.5 = (s32[1536]{0:T(1024)S(1)}, s32[1536]{0:T(1024)}, u32[]{:S(2)}) copy-start(s32[1536]{0:T(1024)} %param.17) | copy-start | bytes 18436
  8.1 18.1 %copy-start.4 = (bf16[2,32,2,256]{3,2,1,0:T(2,128)(2,1)S(1)}, bf16[2,32,2,256]{3,2,1,0:T(2,128)(2,1)}, u32[]{:S(2)}) copy-start(bf16[2,32,2,256]{3,2,1,0:T(2,128)(2,1)} %param.14) | copy-start | bytes 196612
  8.1 18.2 %copy-start.6 = (bf16[2,32,256]{2,1,0:T(8,128)(2,1)S(1)}, bf16[2,32,256]{2,1,0:T(8,128)(2,1)}, u32[]{:S(2)}) copy-start(bf16[2,32,256]{2,1,0:T(8,128)(2,1)} %param.13) | copy-start | bytes 98308
  8.1 82.9 %all-to-all-start = ((bf16[96,64,256]{2,1,0:T(8,128)(2,1)}), bf16[96,64,256]{2,1,0:T(8,128)(2,1)}, u32[]{:S(2)}, u32[]{:S(2)}) async-start(bf16[96,64,256]{2,1,0:T(8,128)(2,1)} %bitcast.149), calls=%async_computation | async-start | bytes 6291456 | tf_op jit(solution)/shard_map/all_to_all | solution.py:69
  93.2 1.1 copy-start.2
  97.6 18.0 %copy-start.3 = (bf16[2,4,2048]{2,1,0:T(4,128)(2,1)S(1)}, bf16[2,4,2048]{2,1,0:T(4,128)(2,1)}, u32[]{:S(2)}) copy-start(bf16[2,4,2048]{2,1,0:T(4,128)(2,1)} %param.20) | copy-start | bytes 98308
  97.6 18.3 %copy-start.7 = (f32[2,2048]{1,0:T(2,128)S(1)}, f32[2,2048]{1,0:T(2,128)}, u32[]{:S(2)}) copy-start(f32[2,2048]{1,0:T(2,128)} %param.22) | copy-start | bytes 49156
  97.7 18.3 %copy-start.8 = (f32[2,2048]{1,0:T(2,128)S(1)}, f32[2,2048]{1,0:T(2,128)}, u32[]{:S(2)}) copy-start(f32[2,2048]{1,0:T(2,128)} %param.21) | copy-start | bytes 49156
  99.1 16.4 %all-to-all-start.1 = ((f32[8,4,2,2048]{3,1,2,0:T(4,128)}), f32[8,4,2,2048]{3,1,2,0:T(4,128)S(1)}, u32[]{:S(2)}, u32[]{:S(2)}) async-start(f32[8,4,2,2048]{3,1,2,0:T(4,128)} %copy.97), calls=%async_computation.1 | async-start | bytes 1048576 | tf_op jit(solution)/shard_map/all_to_all | solution.py:153
  116.1 1.8 collective-permute-start
  117.9 4.1 %collective-permute-start.1 = (bf16[8,2048]{1,0:T(8,128)(2,1)S(1)}, bf16[8,2048]{1,0:T(8,128)(2,1)S(1)}, u32[]{:S(2)}, u32[]{:S(2)}) collective-permute-start(bf16[8,2048]{1,0:T(8,128)(2,1)S(1)} %get-tuple-element.16), channel_id=1, source_target_pairs={{0,2},{1,3},{2,4},{3,5},{4,6},{5,7},{6,0},{7,1},{8,10},{9,11},{10,... | collective-permute-start | bytes 98312 | tf_op jit(solution)/shard_map/ppermute | solution.py:193
  118.3 4.3 %collective-permute-start.2 = (bf16[8,2048]{1,0:T(8,128)(2,1)S(1)}, bf16[8,2048]{1,0:T(8,128)(2,1)S(1)}, u32[]{:S(2)}, u32[]{:S(2)}) collective-permute-start(bf16[8,2048]{1,0:T(8,128)(2,1)S(1)} %get-tuple-element.16), channel_id=1, source_target_pairs={{0,4},{1,5},{2,6},{3,7},{4,0},{5,1},{6,2},{7,3},{8,12},{9,13},{10,... | collective-permute-start | bytes 98312 | tf_op jit(solution)/shard_map/ppermute | solution.py:193
  120.1 3.1 %collective-permute-start.3 = (bf16[8,2048]{1,0:T(8,128)(2,1)S(1)}, bf16[8,2048]{1,0:T(8,128)(2,1)S(1)}, u32[]{:S(2)}, u32[]{:S(2)}) collective-permute-start(bf16[8,2048]{1,0:T(8,128)(2,1)S(1)} %get-tuple-element.16), channel_id=1, source_target_pairs={{0,6},{1,7},{2,0},{3,1},{4,2},{5,3},{6,4},{7,5},{8,14},{9,15},{10,... | collective-permute-start | bytes 98312 | tf_op jit(solution)/shard_map/ppermute | solution.py:193
  123.2 5.8 %collective-permute-start.4 = (bf16[32,2048]{1,0:T(8,128)(2,1)S(1)}, bf16[32,2048]{1,0:T(8,128)(2,1)S(1)}, u32[]{:S(2)}, u32[]{:S(2)}) collective-permute-start(bf16[32,2048]{1,0:T(8,128)(2,1)S(1)} %pad_maximum_fusion), channel_id=1, source_target_pairs={{0,8},{8,16},{16,24},{24,0},{32,40},{40,48},{48,56},{56,32},{64,72... | collective-permute-start | bytes 393224 | tf_op jit(solution)/shard_map/ppermute | solution.py:196
  123.8 6.7 %collective-permute-start.5 = (bf16[32,2048]{1,0:T(8,128)(2,1)S(1)}, bf16[32,2048]{1,0:T(8,128)(2,1)S(1)}, u32[]{:S(2)}, u32[]{:S(2)}) collective-permute-start(bf16[32,2048]{1,0:T(8,128)(2,1)S(1)} %pad_maximum_fusion), channel_id=1, source_target_pairs={{0,16},{8,24},{16,0},{24,8},{32,48},{40,56},{48,32},{56,40},{64,80... | collective-permute-start | bytes 393224 | tf_op jit(solution)/shard_map/ppermute | solution.py:196
  126.1 5.0 %collective-permute-start.6 = (bf16[32,2048]{1,0:T(8,128)(2,1)S(1)}, bf16[32,2048]{1,0:T(8,128)(2,1)S(1)}, u32[]{:S(2)}, u32[]{:S(2)}) collective-permute-start(bf16[32,2048]{1,0:T(8,128)(2,1)S(1)} %pad_maximum_fusion), channel_id=1, source_target_pairs={{0,24},{8,0},{16,8},{24,16},{32,56},{40,32},{48,40},{56,48},{64,88... | collective-permute-start | bytes 393224 | tf_op jit(solution)/shard_map/ppermute | solution.py:196
  131.8 11.7 %collective-permute-start.7 = (bf16[128,2048]{1,0:T(8,128)(2,1)S(1)}, bf16[128,2048]{1,0:T(8,128)(2,1)S(1)}, u32[]{:S(2)}, u32[]{:S(2)}) collective-permute-start(bf16[128,2048]{1,0:T(8,128)(2,1)S(1)} %get-tuple-element.19), channel_id=1, source_target_pairs={{0,32},{8,40},{16,48},{24,56},{32,64},{40,72},{48,80},{56,88},{64,... | collective-permute-start | bytes 1572872 | tf_op jit(solution)/shard_map/ppermute | solution.py:202
  133.9 10.5 %collective-permute-start.8 = (bf16[128,2048]{1,0:T(8,128)(2,1)S(1)}, bf16[128,2048]{1,0:T(8,128)(2,1)S(1)}, u32[]{:S(2)}, u32[]{:S(2)}) collective-permute-start(bf16[128,2048]{1,0:T(8,128)(2,1)S(1)} %get-tuple-element.19), channel_id=1, source_target_pairs={{0,224},{8,232},{16,240},{24,248},{32,0},{40,8},{48,16},{56,24},{6... | collective-permute-start | bytes 1572872 | tf_op jit(solution)/shard_map/ppermute | solution.py:206
  143.5 10.8 %collective-permute-start.9 = (bf16[128,2048]{1,0:T(8,128)(2,1)S(1)}, bf16[128,2048]{1,0:T(8,128)(2,1)S(1)}, u32[]{:S(2)}, u32[]{:S(2)}) collective-permute-start(bf16[128,2048]{1,0:T(8,128)(2,1)S(1)} %collective-permute-done.7), channel_id=1, source_target_pairs={{0,32},{8,40},{16,48},{24,56},{32,64},{40,72},{48,80},{56,88},{64,... | collective-permute-start | bytes 1572872 | tf_op jit(solution)/shard_map/ppermute | solution.py:202
  144.4 12.1 %collective-permute-start.10 = (bf16[128,2048]{1,0:T(8,128)(2,1)S(1)}, bf16[128,2048]{1,0:T(8,128)(2,1)S(1)}, u32[]{:S(2)}, u32[]{:S(2)}) collective-permute-start(bf16[128,2048]{1,0:T(8,128)(2,1)S(1)} %collective-permute-done.8), channel_id=1, source_target_pairs={{0,224},{8,232},{16,240},{24,248},{32,0},{40,8},{48,16},{56,24},{6... | collective-permute-start | bytes 1572872 | tf_op jit(solution)/shard_map/ppermute | solution.py:206
  154.3 10.4 %collective-permute-start.11 = (bf16[128,2048]{1,0:T(8,128)(2,1)S(1)}, bf16[128,2048]{1,0:T(8,128)(2,1)S(1)}, u32[]{:S(2)}, u32[]{:S(2)}) collective-permute-start(bf16[128,2048]{1,0:T(8,128)(2,1)S(1)} %collective-permute-done.9), channel_id=1, source_target_pairs={{0,32},{8,40},{16,48},{24,56},{32,64},{40,72},{48,80},{56,88},{64,... | collective-permute-start | bytes 1572872 | tf_op jit(solution)/shard_map/ppermute | solution.py:202
  155.7 27.2 %copy-start.11 = (s32[8]{0:T(128)S(1)}, s32[8]{0:T(128)}, u32[]{:S(2)}) copy-start(s32[8]{0:T(128)} %constant.235) | copy-start | bytes 100
  155.7 27.6 %copy-start.10 = (s32[1024]{0:T(1024)S(1)}, s32[1024]{0:T(1024)}, u32[]{:S(2)}) copy-start(s32[1024]{0:T(1024)} %param.24) | copy-start | bytes 12292
  156.5 10.4 %collective-permute-start.12 = (bf16[128,2048]{1,0:T(8,128)(2,1)S(1)}, bf16[128,2048]{1,0:T(8,128)(2,1)S(1)}, u32[]{:S(2)}, u32[]{:S(2)}) collective-permute-start(bf16[128,2048]{1,0:T(8,128)(2,1)S(1)} %collective-permute-done.10), channel_id=1, source_target_pairs={{0,224},{8,232},{16,240},{24,248},{32,0},{40,8},{48,16},{56,24},{6... | collective-permute-start | bytes 1572872 | tf_op jit(solution)/shard_map/ppermute | solution.py:206
  164.7 10.5 %collective-permute-start.13 = (bf16[128,2048]{1,0:T(8,128)(2,1)S(1)}, bf16[128,2048]{1,0:T(8,128)(2,1)S(1)}, u32[]{:S(2)}, u32[]{:S(2)}) collective-permute-start(bf16[128,2048]{1,0:T(8,128)(2,1)S(1)} %collective-permute-done.11), channel_id=1, source_target_pairs={{0,32},{8,40},{16,48},{24,56},{32,64},{40,72},{48,80},{56,88},{64,... | collective-permute-start | bytes 1572872 | tf_op jit(solution)/shard_map/ppermute | solution.py:202
  176.1 18.2 %collective-permute-start.14 = (bf16[1024,2048]{1,0:T(8,128)(2,1)}, bf16[1024,2048]{1,0:T(8,128)(2,1)}, u32[]{:S(2)}, u32[]{:S(2)}) collective-permute-start(bf16[1024,2048]{1,0:T(8,128)(2,1)} %constant_dynamic-update-slice_fusion.7), channel_id=1, source_target_pairs={{0,1},{1,0},{2,3},{3,2},{4,5},{5,4},{6,7},{7,6},{8,9},{9,8},{10,11... | collective-permute-start | bytes 12582920 | tf_op jit(solution)/shard_map/ppermute | solution.py:210
  207.5 7.1 %copy-start.1 = (s32[2]{0:T(128)S(1)}, s32[2]{0:T(128)}, u32[]{:S(2)}) copy-start(s32[2]{0:T(128)} %param.18) | copy-start | bytes 28
  211.1 8.2 %all-to-all-start.2 = ((f32[8,1,768]{2,1,0:T(1,128)}), f32[8,1,768]{2,1,0:T(1,128)S(1)}, u32[]{:S(2)}, u32[]{:S(2)}) async-start(f32[8,1,768]{2,1,0:T(1,128)} %reshape.788), calls=%async_computation.2 | async-start | bytes 49152 | tf_op jit(solution)/shard_map/all_to_all | solution.py:244
  221.4 15.5 %all-to-all-start.3 = ((f32[3,2,32,4]{3,1,0,2:T(2,128)}), f32[3,2,32,4]{3,1,0,2:T(2,128)S(1)}, u32[]{:S(2)}, u32[]{:S(2)}) async-start(f32[3,2,32,4]{3,1,0,2:T(2,128)} %copy.110), calls=%async_computation.3 | async-start | bytes 196608 | tf_op jit(solution)/shard_map/all_to_all | solution.py:246

commit v5 on v4

--- a/solution.py
+++ b/solution.py
@@ -198,14 +198,19 @@
     forward, backward = block, block
     chunks = [block]
     z_from = [0]
-    for k in range(1, z_size // 2 + 1):
+    for k in range(1, z_size // 2):
         forward = lax.ppermute(forward, "group", z_shift(1))
         chunks.append(forward)
         z_from.append(k)
-        if k < z_size // 2:
-            backward = lax.ppermute(backward, "group", z_shift(z_size - 1))
-            chunks.append(backward)
-            z_from.append(z_size - k)
+        backward = lax.ppermute(backward, "group", z_shift(z_size - 1))
+        chunks.append(backward)
+        z_from.append(z_size - k)
+    split = block.shape[0] // 2
+    chunks.append(jnp.concatenate([
+        lax.ppermute(forward[:split], "group", z_shift(1)),
+        lax.ppermute(backward[split:], "group", z_shift(z_size - 1)),
+    ], 0))
+    z_from.append(z_size // 2)
     own_model = jnp.concatenate(chunks, 0)
     other_model = lax.ppermute(own_model, "tensor", swap)
     z_from = jnp.array(z_from, dtype=jnp.int32)

time: 238 us -> 237 us (level)
  waiting for transfers between devices: 118 us -> 112 us
  starting transfers between devices: 52.1 us -> 55.1 us
    ppermute x4 -> x3, waiting for transfers between devices: 29.8 us -> 21.5 us  [per_device(): forward = lax.ppermute(forward, 'group', z_shift(1))]
    ppermute x0 -> x2, waiting for transfers between devices: none -> 3.18 us  [the longest x1 3.17 us: per_device(): lax.ppermute(forward[:split], 'group', z_shift(1))]
    ppermute x0 -> x2, starting transfers between devices: none -> 2.83 us  [the longest x1 2.29 us: per_device(): lax.ppermute(backward[split:], 'group', z_shift(z_size - 1))]
    unnamed x38 -> x39, local copies, waits for them, and re-layouts: 10.5 us -> 11.2 us
  transfers between devices with their start and end apart: 19 -> 20, of which waited for: 13 -> 13; matrix products, arithmetic and copies ran while one was open for 12% -> 13% of each run, Pallas kernels for 0% -> 0%
where the time goes in v5:
time: 237 us; the launch traced here: 236 us
  waiting for transfers between devices  112 us (47%)
  starting transfers between devices  55.1 us (23%)
  local copies, waits for them, and re-layouts  29.7 us (13%)
  matrix products  22.7 us (10%)
  other arithmetic  15.6 us (7%)
    all_to_all x1, waiting for transfers between devices, per_device(): lax.all_to_all(outgoing.reshape(buffer, -1, flat_width), 'group', split_a...  61.7 us
    ppermute x3, waiting for transfers between devices, per_device(): forward = lax.ppermute(forward, 'group', z_shift(1))  21.5 us
    dot_general x2, matrix products, local_stats(): logits = jnp.dot(rows, weights, preferred_element_type=jnp.float32)  16.7 us
    all_to_all x1, starting transfers between devices, per_device(): lax.all_to_all(outgoing.reshape(buffer, -1, flat_width), 'group', split_a...  12.3 us
    unnamed x39, local copies, waits for them, and re-layouts  11.2 us
    all_to_all x1, waiting for transfers between devices, per_device(): lax.all_to_all(partial.reshape(shards, rows_local, 2, width), 'tensor', 0...  9.48 us
    all_to_all x1, waiting for transfers between devices, per_device(): lax.all_to_all(jnp.stack([peak, total, chosen]), 'group', 2, 2, tiled=True)  9.06 us
    all_to_all x1, starting transfers between devices, per_device(): lax.all_to_all(jnp.stack([peak, total, chosen]), 'group', 2, 2, tiled=True)  7.02 us
  transfers between devices with their start and end apart: 20, of which 13 were waited for; matrix products, arithmetic and copies ran while one was open for 13% of the time, Pallas kernels for 0%

profile of v5, /device:TPU:1, one launch (start us, length us, event | category | flops | bytes accessed | tf_op | source)
XLA Modules:
  0.0 236.1 jit_solution(4020720398804278157)
XLA Ops:
  0.0 0.9 fusion.81
  1.1 0.8 multiply_add_fusion
  1.8 2.8 %convert_bitcast_fusion = bf16[96,2,2,16,256]{4,0,1,3,2:T(8,128)(2,1)S(1)} fusion(bf16[2,48,16,2,256]{4,3,2,1,0:T(2,128)(2,1)} %param.15, s32[48]{0:T(128)S(1)} %multiply_add_fusion), kind=kOutput, calls=%fused_computation.16 | convolution fusion | flops 152572416 | bytes 4718784 | tf_op jit(solution)/shard_map/sp,mpjcx->scmjx/dot_general | solution.py:66
  4.6 3.5 %copy.88 = bf16[96,2,2,16,256]{4,3,2,1,0:T(8,128)(2,1)} copy(bf16[96,2,2,16,256]{4,0,1,3,2:T(8,128)(2,1)S(1)} %convert_bitcast_fusion) | data formatting | bytes 6291456 | tf_op jit(solution)/shard_map/convert_element_type | solution.py:68
  8.1 12.3 %all-to-all-start = ((bf16[96,64,256]{2,1,0:T(8,128)(2,1)}), bf16[96,64,256]{2,1,0:T(8,128)(2,1)}, u32[]{:S(2)}, u32[]{:S(2)}) async-start(bf16[96,64,256]{2,1,0:T(8,128)(2,1)} %bitcast.149), calls=%async_computation | async-start | bytes 6291456 | tf_op jit(solution)/shard_map/all_to_all | solution.py:69
  20.5 0.6 convert_reduce_fusion
  22.1 1.2 fusion.80
  23.3 0.6 fusion.100
  24.8 1.4 convert_multiply_fusion.3
  26.8 2.4 %convert_multiply_fusion.1 = (f32[32,96,16]{0,2,1:T(8,128)}, f32[32,96,16]{0,2,1:T(8,128)S(1)}) fusion(s32[96,16]{1,0:T(8,128)S(1)} %iota_add_fusion, s32[32]{0:T(128)S(1)} %fusion.80, f32[]{:T(128)} %bitcast.12, f32[]{:T(128)} %bitcast.24), kind=kLoop, calls=%fused_computation.54 | loop fusion | flops 196608 | bytes 399496 | tf_op jit(solution)/shard_map/mul | solution.py:133
  29.2 61.7 %all-to-all-done = bf16[96,64,256]{2,1,0:T(8,128)(2,1)} async-done(((bf16[96,64,256]{2,1,0:T(8,128)(2,1)}), bf16[96,64,256]{2,1,0:T(8,128)(2,1)}, u32[]{:S(2)}, u32[]{:S(2)}) %all-to-all-start) | async-done | bytes 3145760 | tf_op jit(solution)/shard_map/all_to_all | solution.py:69
  91.0 2.2 fusion.98
  93.5 0.8 copy-done.2
  95.9 0.7 fusion.9
  98.3 0.8 copy.97
  99.1 6.9 %all-to-all-start.1 = ((f32[8,4,2,2048]{3,1,2,0:T(4,128)}), f32[8,4,2,2048]{3,1,2,0:T(4,128)S(1)}, u32[]{:S(2)}, u32[]{:S(2)}) async-start(f32[8,4,2,2048]{3,1,2,0:T(4,128)} %copy.97), calls=%async_computation.1 | async-start | bytes 1048576 | tf_op jit(solution)/shard_map/all_to_all | solution.py:153
  106.1 9.5 %all-to-all-done.1 = f32[8,4,2,2048]{3,1,2,0:T(4,128)S(1)} async-done(((f32[8,4,2,2048]{3,1,2,0:T(4,128)}), f32[8,4,2,2048]{3,1,2,0:T(4,128)S(1)}, u32[]{:S(2)}, u32[]{:S(2)}) %all-to-all-start.1) | async-done | bytes 524320 | tf_op jit(solution)/shard_map/all_to_all | solution.py:153
  116.1 1.0 collective-permute-start
  117.0 0.8 collective-permute-done
  118.3 1.8 collective-permute-start.2
  120.1 0.7 collective-permute-start.3
  120.8 0.6 constant_dynamic-update-slice_fusion.21
  122.6 0.6 collective-permute-done.3
  123.8 2.4 %collective-permute-start.5 = (bf16[32,2048]{1,0:T(8,128)(2,1)S(1)}, bf16[32,2048]{1,0:T(8,128)(2,1)S(1)}, u32[]{:S(2)}, u32[]{:S(2)}) collective-permute-start(bf16[32,2048]{1,0:T(8,128)(2,1)S(1)} %pad_maximum_fusion), channel_id=1, source_target_pairs={{0,16},{8,24},{16,0},{24,8},{32,48},{40,56},{48,32},{56,40},{64,80... | collective-permute-start | bytes 393224 | tf_op jit(solution)/shard_map/ppermute | solution.py:196
  126.1 1.0 collective-permute-start.6
  127.2 0.6 constant_dynamic-update-slice_fusion.5
  127.8 0.6 constant_dynamic-update-slice_fusion.4
  128.4 0.6 constant_dynamic-update-slice_fusion.3
  129.0 0.7 constant_dynamic-update-slice_fusion.2
  129.7 0.8 collective-permute-done.5
  130.5 0.7 constant_dynamic-update-slice_fusion.1
  131.2 0.7 constant_dynamic-update-slice_fusion
  131.8 2.1 collective-permute-start.7
  134.5 9.0 %collective-permute-done.7 = bf16[128,2048]{1,0:T(8,128)(2,1)S(1)} collective-permute-done((bf16[128,2048]{1,0:T(8,128)(2,1)S(1)}, bf16[128,2048]{1,0:T(8,128)(2,1)S(1)}, u32[]{:S(2)}, u32[]{:S(2)}) %collective-permute-start.7) | collective-permute-done | bytes 524320 | tf_op jit(solution)/shard_map/ppermute | solution.py:202
  143.5 0.9 collective-permute-start.9
  144.4 1.8 collective-permute-start.10
  146.2 0.9 constant_dynamic-update-slice_fusion.14
  147.1 7.3 %collective-permute-done.9 = bf16[128,2048]{1,0:T(8,128)(2,1)S(1)} collective-permute-done((bf16[128,2048]{1,0:T(8,128)(2,1)S(1)}, bf16[128,2048]{1,0:T(8,128)(2,1)S(1)}, u32[]{:S(2)}, u32[]{:S(2)}) %collective-permute-start.9) | collective-permute-done | bytes 524320 | tf_op jit(solution)/shard_map/ppermute | solution.py:202
  154.8 2.2 collective-permute-start.12
  157.0 0.8 constant_dynamic-update-slice_fusion.13
  157.9 0.8 constant_dynamic-update-slice_fusion.12
  158.7 0.8 constant_dynamic-update-slice_fusion.11
  159.6 5.2 %collective-permute-done.11 = bf16[128,2048]{1,0:T(8,128)(2,1)S(1)} collective-permute-done((bf16[128,2048]{1,0:T(8,128)(2,1)S(1)}, bf16[128,2048]{1,0:T(8,128)(2,1)S(1)}, u32[]{:S(2)}, u32[]{:S(2)}) %collective-permute-start.11) | collective-permute-done | bytes 524320 | tf_op jit(solution)/shard_map/ppermute | solution.py:202
  165.3 2.3 collective-permute-start.14
  167.6 0.9 constant_dynamic-update-slice_fusion.10
  168.5 0.8 constant_dynamic-update-slice_fusion.9
  169.3 3.2 %collective-permute-done.13 = bf16[64,2048]{1,0:T(8,128)(2,1)S(1)} collective-permute-done((bf16[64,2048]{1,0:T(8,128)(2,1)S(1)}, bf16[64,2048]{1,0:T(8,128)(2,1)S(1)}, u32[]{:S(2)}, u32[]{:S(2)}) %collective-permute-start.13) | collective-permute-done | bytes 262176 | tf_op jit(solution)/shard_map/ppermute | solution.py:210
  172.5 0.7 constant_dynamic-update-slice_fusion.8
  173.2 0.7 constant_dynamic-update-slice_fusion.7
  173.9 6.7 %collective-permute-start.15 = (bf16[1024,2048]{1,0:T(8,128)(2,1)}, bf16[1024,2048]{1,0:T(8,128)(2,1)}, u32[]{:S(2)}, u32[]{:S(2)}) collective-permute-start(bf16[1024,2048]{1,0:T(8,128)(2,1)} %constant_dynamic-update-slice_fusion.7), channel_id=1, source_target_pairs={{0,1},{1,0},{2,3},{3,2},{4,5},{5,4},{6,7},{7,6},{8,9},{9,8},{10,11... | collective-permute-start | bytes 12582920 | tf_op jit(solution)/shard_map/ppermute | solution.py:215
  181.2 1.0 gather_fusion.1
  182.5 0.9 scatter_custom_fusion
  183.5 8.4 %fusion.106 = (f32[1024]{0:T(1024)S(1)}, f32[1024,768]{0,1:T(8,128)}) fusion(bf16[1024,2048]{1,0:T(8,128)(2,1)} %constant_dynamic-update-slice_fusion.7, bf16[2,2048,768]{2,1,0:T(8,128)(2,1)} %param.23, s32[]{:T(128)S(6)} %select_n.338), kind=kOutput, calls=%fused_computation.249 | convolution fusion | flops 3222010880 | bytes 10489860 | tf_op jit(solution)/shard_map/dot_general | solution.py:229
  192.1 8.3 %fusion.107 = (f32[1024]{0:T(1024)S(1)}, f32[1024,768]{0,1:T(8,128)}) fusion(bf16[1024,2048]{1,0:T(8,128)(2,1)} %collective-permute-done.15, bf16[2,2048,768]{2,1,0:T(8,128)(2,1)} %param.23, s32[]{:T(128)S(6)} %select_n.339), kind=kOutput, calls=%fused_computation.250 | convolution fusion | flops 3222010880 | bytes 10489860 | tf_op jit(solution)/shard_map/dot_general | solution.py:229
  200.5 4.4 %exponential_reduce_fusion.1 = (f32[1024]{0:T(1024)S(1)}, f32[1024]{0:T(1024)S(1)}, f32[1024]{0:T(1024)S(1)}, f32[1024]{0:T(1024)S(1)}) fusion(f32[1024,768]{0,1:T(8,128)} %get-tuple-element.58, f32[1024]{0:T(1024)S(1)} %get-tuple-element.57, s32[1024]{0:T(1024)S(1)} %sub.286, f32[1024,768]{0,1:T(8,128)} %get-tuple-element.60, f32[1024]{0:T(1024)S(1)} %get-tuple-element.59), kind=kLoop, calls=%fused_computation.14 | loop fusion | flops 7073792 | bytes 6320128 | tf_op jit(solution)/shard_map/reduce_sum | solution.py:231
  206.3 0.8 gather_fusion.2
  208.1 0.7 reshape.788
  208.9 3.6 %all-to-all-start.2 = ((f32[8,1,768]{2,1,0:T(1,128)}), f32[8,1,768]{2,1,0:T(1,128)S(1)}, u32[]{:S(2)}, u32[]{:S(2)}) async-start(f32[8,1,768]{2,1,0:T(1,128)} %reshape.788), calls=%async_computation.2 | async-start | bytes 49152 | tf_op jit(solution)/shard_map/all_to_all | solution.py:249
  212.5 0.6 gather_fusion
  213.1 4.0 %all-to-all-done.2 = f32[8,1,768]{2,1,0:T(1,128)S(1)} async-done(((f32[8,1,768]{2,1,0:T(1,128)}), f32[8,1,768]{2,1,0:T(1,128)S(1)}, u32[]{:S(2)}, u32[]{:S(2)}) %all-to-all-start.2) | async-done | bytes 24608 | tf_op jit(solution)/shard_map/all_to_all | solution.py:249
  217.6 0.7 reduce.11
  218.5 0.7 copy.110
  219.3 7.0 %all-to-all-start.3 = ((f32[3,2,32,4]{3,1,0,2:T(2,128)}), f32[3,2,32,4]{3,1,0,2:T(2,128)S(1)}, u32[]{:S(2)}, u32[]{:S(2)}) async-start(f32[3,2,32,4]{3,1,0,2:T(2,128)} %copy.110), calls=%async_computation.3 | async-start | bytes 196608 | tf_op jit(solution)/shard_map/all_to_all | solution.py:251
  226.3 9.1 %all-to-all-done.3 = f32[3,2,32,4]{3,1,0,2:T(2,128)S(1)} async-done(((f32[3,2,32,4]{3,1,0,2:T(2,128)}), f32[3,2,32,4]{3,1,0,2:T(2,128)S(1)}, u32[]{:S(2)}, u32[]{:S(2)}) %all-to-all-start.3) | async-done | bytes 3104 | tf_op jit(solution)/shard_map/all_to_all | solution.py:251
  (138 shorter events, 15.5 us)
Async XLA Ops:
  0.0 97.6 %copy-start = (bf16[2,256,2048]{2,1,0:T(8,128)(2,1)S(1)}, bf16[2,256,2048]{2,1,0:T(8,128)(2,1)}, u32[]{:S(2)}) copy-start(bf16[2,256,2048]{2,1,0:T(8,128)(2,1)} %param.19) | copy-start | bytes 6291460
  8.1 12.3 %copy-start.9 = (s32[1536,1]{0,1:T(1,128)S(1)}, s32[1536,1]{0,1:T(1,128)}, u32[]{:S(2)}) copy-start(s32[1536,1]{0,1:T(1,128)} %param.16) | copy-start | bytes 18436
  8.1 13.2 %copy-start.5 = (s32[1536]{0:T(1024)S(1)}, s32[1536]{0:T(1024)}, u32[]{:S(2)}) copy-start(s32[1536]{0:T(1024)} %param.17) | copy-start | bytes 18436
  8.1 18.1 %copy-start.4 = (bf16[2,32,2,256]{3,2,1,0:T(2,128)(2,1)S(1)}, bf16[2,32,2,256]{3,2,1,0:T(2,128)(2,1)}, u32[]{:S(2)}) copy-start(bf16[2,32,2,256]{3,2,1,0:T(2,128)(2,1)} %param.14) | copy-start | bytes 196612
  8.1 18.2 %copy-start.6 = (bf16[2,32,256]{2,1,0:T(8,128)(2,1)S(1)}, bf16[2,32,256]{2,1,0:T(8,128)(2,1)}, u32[]{:S(2)}) copy-start(bf16[2,32,256]{2,1,0:T(8,128)(2,1)} %param.13) | copy-start | bytes 98308
  8.1 82.9 %all-to-all-start = ((bf16[96,64,256]{2,1,0:T(8,128)(2,1)}), bf16[96,64,256]{2,1,0:T(8,128)(2,1)}, u32[]{:S(2)}, u32[]{:S(2)}) async-start(bf16[96,64,256]{2,1,0:T(8,128)(2,1)} %bitcast.149), calls=%async_computation | async-start | bytes 6291456 | tf_op jit(solution)/shard_map/all_to_all | solution.py:69
  93.2 1.1 copy-start.2
  97.6 18.0 %copy-start.3 = (bf16[2,4,2048]{2,1,0:T(4,128)(2,1)S(1)}, bf16[2,4,2048]{2,1,0:T(4,128)(2,1)}, u32[]{:S(2)}) copy-start(bf16[2,4,2048]{2,1,0:T(4,128)(2,1)} %param.20) | copy-start | bytes 98308
  97.6 18.3 %copy-start.7 = (f32[2,2048]{1,0:T(2,128)S(1)}, f32[2,2048]{1,0:T(2,128)}, u32[]{:S(2)}) copy-start(f32[2,2048]{1,0:T(2,128)} %param.22) | copy-start | bytes 49156
  97.7 18.3 %copy-start.8 = (f32[2,2048]{1,0:T(2,128)S(1)}, f32[2,2048]{1,0:T(2,128)}, u32[]{:S(2)}) copy-start(f32[2,2048]{1,0:T(2,128)} %param.21) | copy-start | bytes 49156
  99.1 16.4 %all-to-all-start.1 = ((f32[8,4,2,2048]{3,1,2,0:T(4,128)}), f32[8,4,2,2048]{3,1,2,0:T(4,128)S(1)}, u32[]{:S(2)}, u32[]{:S(2)}) async-start(f32[8,4,2,2048]{3,1,2,0:T(4,128)} %copy.97), calls=%async_computation.1 | async-start | bytes 1048576 | tf_op jit(solution)/shard_map/all_to_all | solution.py:153
  116.1 1.8 collective-permute-start
  117.9 4.1 %collective-permute-start.1 = (bf16[8,2048]{1,0:T(8,128)(2,1)S(1)}, bf16[8,2048]{1,0:T(8,128)(2,1)S(1)}, u32[]{:S(2)}, u32[]{:S(2)}) collective-permute-start(bf16[8,2048]{1,0:T(8,128)(2,1)S(1)} %get-tuple-element.16), channel_id=1, source_target_pairs={{0,2},{1,3},{2,4},{3,5},{4,6},{5,7},{6,0},{7,1},{8,10},{9,11},{10,... | collective-permute-start | bytes 98312 | tf_op jit(solution)/shard_map/ppermute | solution.py:193
  118.3 4.3 %collective-permute-start.2 = (bf16[8,2048]{1,0:T(8,128)(2,1)S(1)}, bf16[8,2048]{1,0:T(8,128)(2,1)S(1)}, u32[]{:S(2)}, u32[]{:S(2)}) collective-permute-start(bf16[8,2048]{1,0:T(8,128)(2,1)S(1)} %get-tuple-element.16), channel_id=1, source_target_pairs={{0,4},{1,5},{2,6},{3,7},{4,0},{5,1},{6,2},{7,3},{8,12},{9,13},{10,... | collective-permute-start | bytes 98312 | tf_op jit(solution)/shard_map/ppermute | solution.py:193
  120.1 3.1 %collective-permute-start.3 = (bf16[8,2048]{1,0:T(8,128)(2,1)S(1)}, bf16[8,2048]{1,0:T(8,128)(2,1)S(1)}, u32[]{:S(2)}, u32[]{:S(2)}) collective-permute-start(bf16[8,2048]{1,0:T(8,128)(2,1)S(1)} %get-tuple-element.16), channel_id=1, source_target_pairs={{0,6},{1,7},{2,0},{3,1},{4,2},{5,3},{6,4},{7,5},{8,14},{9,15},{10,... | collective-permute-start | bytes 98312 | tf_op jit(solution)/shard_map/ppermute | solution.py:193
  123.2 5.8 %collective-permute-start.4 = (bf16[32,2048]{1,0:T(8,128)(2,1)S(1)}, bf16[32,2048]{1,0:T(8,128)(2,1)S(1)}, u32[]{:S(2)}, u32[]{:S(2)}) collective-permute-start(bf16[32,2048]{1,0:T(8,128)(2,1)S(1)} %pad_maximum_fusion), channel_id=1, source_target_pairs={{0,8},{8,16},{16,24},{24,0},{32,40},{40,48},{48,56},{56,32},{64,72... | collective-permute-start | bytes 393224 | tf_op jit(solution)/shard_map/ppermute | solution.py:196
  123.8 6.7 %collective-permute-start.5 = (bf16[32,2048]{1,0:T(8,128)(2,1)S(1)}, bf16[32,2048]{1,0:T(8,128)(2,1)S(1)}, u32[]{:S(2)}, u32[]{:S(2)}) collective-permute-start(bf16[32,2048]{1,0:T(8,128)(2,1)S(1)} %pad_maximum_fusion), channel_id=1, source_target_pairs={{0,16},{8,24},{16,0},{24,8},{32,48},{40,56},{48,32},{56,40},{64,80... | collective-permute-start | bytes 393224 | tf_op jit(solution)/shard_map/ppermute | solution.py:196
  126.1 5.0 %collective-permute-start.6 = (bf16[32,2048]{1,0:T(8,128)(2,1)S(1)}, bf16[32,2048]{1,0:T(8,128)(2,1)S(1)}, u32[]{:S(2)}, u32[]{:S(2)}) collective-permute-start(bf16[32,2048]{1,0:T(8,128)(2,1)S(1)} %pad_maximum_fusion), channel_id=1, source_target_pairs={{0,24},{8,0},{16,8},{24,16},{32,56},{40,32},{48,40},{56,48},{64,88... | collective-permute-start | bytes 393224 | tf_op jit(solution)/shard_map/ppermute | solution.py:196
  131.8 11.7 %collective-permute-start.7 = (bf16[128,2048]{1,0:T(8,128)(2,1)S(1)}, bf16[128,2048]{1,0:T(8,128)(2,1)S(1)}, u32[]{:S(2)}, u32[]{:S(2)}) collective-permute-start(bf16[128,2048]{1,0:T(8,128)(2,1)S(1)} %get-tuple-element.19), channel_id=1, source_target_pairs={{0,32},{8,40},{16,48},{24,56},{32,64},{40,72},{48,80},{56,88},{64,... | collective-permute-start | bytes 1572872 | tf_op jit(solution)/shard_map/ppermute | solution.py:202
  133.9 10.5 %collective-permute-start.8 = (bf16[128,2048]{1,0:T(8,128)(2,1)S(1)}, bf16[128,2048]{1,0:T(8,128)(2,1)S(1)}, u32[]{:S(2)}, u32[]{:S(2)}) collective-permute-start(bf16[128,2048]{1,0:T(8,128)(2,1)S(1)} %get-tuple-element.19), channel_id=1, source_target_pairs={{0,224},{8,232},{16,240},{24,248},{32,0},{40,8},{48,16},{56,24},{6... | collective-permute-start | bytes 1572872 | tf_op jit(solution)/shard_map/ppermute | solution.py:205
  143.5 10.8 %collective-permute-start.9 = (bf16[128,2048]{1,0:T(8,128)(2,1)S(1)}, bf16[128,2048]{1,0:T(8,128)(2,1)S(1)}, u32[]{:S(2)}, u32[]{:S(2)}) collective-permute-start(bf16[128,2048]{1,0:T(8,128)(2,1)S(1)} %collective-permute-done.7), channel_id=1, source_target_pairs={{0,32},{8,40},{16,48},{24,56},{32,64},{40,72},{48,80},{56,88},{64,... | collective-permute-start | bytes 1572872 | tf_op jit(solution)/shard_map/ppermute | solution.py:202
  144.4 10.4 %collective-permute-start.10 = (bf16[128,2048]{1,0:T(8,128)(2,1)S(1)}, bf16[128,2048]{1,0:T(8,128)(2,1)S(1)}, u32[]{:S(2)}, u32[]{:S(2)}) collective-permute-start(bf16[128,2048]{1,0:T(8,128)(2,1)S(1)} %collective-permute-done.8), channel_id=1, source_target_pairs={{0,224},{8,232},{16,240},{24,248},{32,0},{40,8},{48,16},{56,24},{6... | collective-permute-start | bytes 1572872 | tf_op jit(solution)/shard_map/ppermute | solution.py:205
  154.3 10.4 %collective-permute-start.11 = (bf16[128,2048]{1,0:T(8,128)(2,1)S(1)}, bf16[128,2048]{1,0:T(8,128)(2,1)S(1)}, u32[]{:S(2)}, u32[]{:S(2)}) collective-permute-start(bf16[128,2048]{1,0:T(8,128)(2,1)S(1)} %collective-permute-done.9), channel_id=1, source_target_pairs={{0,32},{8,40},{16,48},{24,56},{32,64},{40,72},{48,80},{56,88},{64,... | collective-permute-start | bytes 1572872 | tf_op jit(solution)/shard_map/ppermute | solution.py:202
  154.8 10.5 %collective-permute-start.12 = (bf16[128,2048]{1,0:T(8,128)(2,1)S(1)}, bf16[128,2048]{1,0:T(8,128)(2,1)S(1)}, u32[]{:S(2)}, u32[]{:S(2)}) collective-permute-start(bf16[128,2048]{1,0:T(8,128)(2,1)S(1)} %collective-permute-done.10), channel_id=1, source_target_pairs={{0,224},{8,232},{16,240},{24,248},{32,0},{40,8},{48,16},{56,24},{6... | collective-permute-start | bytes 1572872 | tf_op jit(solution)/shard_map/ppermute | solution.py:205
  157.9 22.8 %copy-start.11 = (s32[8]{0:T(128)S(1)}, s32[8]{0:T(128)}, u32[]{:S(2)}) copy-start(s32[8]{0:T(128)} %constant.235) | copy-start | bytes 100
  157.9 23.2 %copy-start.10 = (s32[1024]{0:T(1024)S(1)}, s32[1024]{0:T(1024)}, u32[]{:S(2)}) copy-start(s32[1024]{0:T(1024)} %param.24) | copy-start | bytes 12292
  164.7 7.7 %collective-permute-start.13 = (bf16[64,2048]{1,0:T(8,128)(2,1)S(1)}, bf16[64,2048]{1,0:T(8,128)(2,1)S(1)}, u32[]{:S(2)}, u32[]{:S(2)}) collective-permute-start(bf16[64,2048]{1,0:T(8,128)(2,1)S(1)} %slice.105), channel_id=1, source_target_pairs={{0,32},{8,40},{16,48},{24,56},{32,64},{40,72},{48,80},{56,88},{64,... | collective-permute-start | bytes 786440 | tf_op jit(solution)/shard_map/ppermute | solution.py:210
  165.3 7.9 %collective-permute-start.14 = (bf16[64,2048]{1,0:T(8,128)(2,1)S(1)}, bf16[64,2048]{1,0:T(8,128)(2,1)S(1)}, u32[]{:S(2)}, u32[]{:S(2)}) collective-permute-start(bf16[64,2048]{1,0:T(8,128)(2,1)S(1)} %slice.106), channel_id=1, source_target_pairs={{0,224},{8,232},{16,240},{24,248},{32,0},{40,8},{48,16},{56,24},{6... | collective-permute-start | bytes 786440 | tf_op jit(solution)/shard_map/ppermute | solution.py:211
  173.9 18.2 %collective-permute-start.15 = (bf16[1024,2048]{1,0:T(8,128)(2,1)}, bf16[1024,2048]{1,0:T(8,128)(2,1)}, u32[]{:S(2)}, u32[]{:S(2)}) collective-permute-start(bf16[1024,2048]{1,0:T(8,128)(2,1)} %constant_dynamic-update-slice_fusion.7), channel_id=1, source_target_pairs={{0,1},{1,0},{2,3},{3,2},{4,5},{5,4},{6,7},{7,6},{8,9},{9,8},{10,11... | collective-permute-start | bytes 12582920 | tf_op jit(solution)/shard_map/ppermute | solution.py:215
  205.3 7.2 %copy-start.1 = (s32[2]{0:T(128)S(1)}, s32[2]{0:T(128)}, u32[]{:S(2)}) copy-start(s32[2]{0:T(128)} %param.18) | copy-start | bytes 28
  208.9 8.2 %all-to-all-start.2 = ((f32[8,1,768]{2,1,0:T(1,128)}), f32[8,1,768]{2,1,0:T(1,128)S(1)}, u32[]{:S(2)}, u32[]{:S(2)}) async-start(f32[8,1,768]{2,1,0:T(1,128)} %reshape.788), calls=%async_computation.2 | async-start | bytes 49152 | tf_op jit(solution)/shard_map/all_to_all | solution.py:249
  219.3 16.1 %all-to-all-start.3 = ((f32[3,2,32,4]{3,1,0,2:T(2,128)}), f32[3,2,32,4]{3,1,0,2:T(2,128)S(1)}, u32[]{:S(2)}, u32[]{:S(2)}) async-start(f32[3,2,32,4]{3,1,0,2:T(2,128)} %copy.110), calls=%async_computation.3 | async-start | bytes 196608 | tf_op jit(solution)/shard_map/all_to_all | solution.py:251
